TPU v7x, 1024 devices: a whole 8x8x8 slice. The times are simulated.
1024 devices in a mesh: rows: 64 (over x, y), chip: 16 (over z, core).
Axes of the slice: x: 8, y: 8, z: 8, core: 2. Of those that a mesh axis runs over, the one named last changes fastest.
Arguments:
- spectra: float32 [262144, 512], P(('rows', 'chip')), may hold values from -250 to 250
Outputs:
- whitened: float32 [262144, 512], P(('rows', 'chip'))
- triangle: float32 [512, 512], replicated
All inputs are finite; a program needn't handle non-finite values.
Results may differ from a plain program's by a relative error of at most 0.000055.
Values sent between devices are 32-bit elements; how exact they have to be, the bound alone decides.
No kernel may reach another device: no remote copies, remote signals or barrier semaphores. Data moves between devices by JAX's collectives and lax.ppermute only.
A program may use at most 32 MiB of HBM per device.

v0:
```python
import math

import jax
import jax.numpy as jnp
from jax import lax
from jax.sharding import PartitionSpec as P


def summed_gram(block):
    gram = lax.dot_general(
        block,
        block,
        (((0,), (0,)), ((), ())),
        precision=lax.Precision.HIGHEST,
        preferred_element_type=jnp.float32,
    )
    return lax.psum(gram, ("rows", "chip"))


def on_device(spectra):
    total_rows = lax.axis_size("rows") * lax.axis_size("chip") * spectra.shape[0]
    lower = jnp.linalg.cholesky(summed_gram(spectra))
    basis = lax.linalg.triangular_solve(
        lower, spectra, left_side=False, lower=True, transpose_a=True
    )
    factor_scale = math.sqrt(total_rows)
    return (basis * factor_scale, lower.T / factor_scale)


def solution(mesh):
    return jax.shard_map(
        on_device,
        mesh=mesh,
        in_specs=(P(("rows", "chip"), None),),
        out_specs=(P(("rows", "chip"), None), P()),
        check_vma=False,
    )
```

profile of v0, /device:TPU:1, one launch (start us, length us, event | category | flops | bytes accessed | tf_op | source)
XLA Modules:
  0.0 471.1 jit_solution(14144385780720443078)
XLA Ops:
  7.2 0.0 all-reduce.3.cloned.1.call-start
  7.2 3.3 fusion.32
  10.5 0.0 all-reduce.3.cloned.1.call-update
  10.6 307.9 %all-reduce.3.cloned.1.call-done = f32[512,512]{0,1:T(8,128)} async-done(((f32[512,512]{0,1:T(8,128)}), f32[512,512]{0,1:T(8,128)}) %all-reduce.3.cloned.1.call-update) | async-done | bytes 1048592 | tf_op jit(solution)/shard_map/psum | solution.py:17
  318.5 1.6 copy.4
  320.1 0.2 fusion
  320.4 11.7 %cholesky.104 = f32[128,128]{1,0:T(8,128)S(1)} custom-call(f32[128,128]{1,0:T(8,128)S(1)} %cholesky.266), custom_call_target="Cholesky" | custom-call | tf_op jit(solution)/shard_map/jit(cholesky)/cholesky | solution.py:22
  332.1 9.8 %custom-call.30 = f32[1,128,128]{1,2,0:T(8,128)S(1)} custom-call(f32[1,128,128]{2,1,0:T(8,128)S(1)} %get-tuple-element.33), custom_call_target="InvertDiagBlocksLowerTriangular" | custom-call | tf_op jit(solution)/shard_map/jit(cholesky)/cholesky | solution.py:22
  342.0 0.1 cholesky.224
  342.1 0.3 constant_dynamic-update-slice_fusion.3
  342.4 0.3 convolution_subtract_fusion
  342.8 11.7 %cholesky.217 = f32[128,128]{1,0:T(8,128)S(1)} custom-call(f32[128,128]{1,0:T(8,128)S(1)} %cholesky.270), custom_call_target="Cholesky" | custom-call | tf_op jit(solution)/shard_map/jit(cholesky)/cholesky | solution.py:22
  354.5 0.2 select_reduce_fusion.2
  354.7 9.8 %custom-call.31 = f32[1,128,128]{1,2,0:T(8,128)S(1)} custom-call(f32[1,128,128]{2,1,0:T(8,128)S(1)} %get-tuple-element.30), custom_call_target="InvertDiagBlocksLowerTriangular" | custom-call | tf_op jit(solution)/shard_map/jit(cholesky)/cholesky | solution.py:22
  364.5 0.3 convolution_dynamic-update-slice_fusion
  364.8 0.4 convolution_subtract_fusion.3
  365.2 11.7 %cholesky.238 = f32[128,128]{1,0:T(8,128)S(1)} custom-call(f32[128,128]{1,0:T(8,128)S(1)} %cholesky.275), custom_call_target="Cholesky" | custom-call | tf_op jit(solution)/shard_map/jit(cholesky)/cholesky | solution.py:22
  376.9 0.7 compare_reduce_fusion.1
  377.6 9.8 %custom-call.32 = f32[1,128,128]{1,2,0:T(8,128)S(1)} custom-call(f32[1,128,128]{2,1,0:T(8,128)S(1)} %get-tuple-element.27), custom_call_target="InvertDiagBlocksLowerTriangular" | custom-call | tf_op jit(solution)/shard_map/jit(cholesky)/cholesky | solution.py:22
  387.4 0.2 convolution_dynamic-update-slice_fusion.1
  387.7 0.4 convolution_subtract_fusion.5
  388.0 11.9 %cholesky.255 = f32[128,128]{1,0:T(8,128)S(1)} custom-call(f32[128,128]{1,0:T(8,128)S(1)} %convolution_subtract_fusion.5), custom_call_target="Cholesky" | custom-call | tf_op jit(solution)/shard_map/jit(cholesky)/cholesky | solution.py:22
  400.0 0.6 compare_reduce_fusion
  400.6 0.7 compare_reduce_fusion.2
  403.8 1.2 multiply_bitcast_fusion
  405.1 11.7 %while.1 = (s32[]{:T(128)}, f32[512,512]{1,0:T(8,128)}, s32[4,2]{0,1:T(2,128)S(1)}, f32[4,128,128]{2,1,0:T(8,128)S(1)}, s32[]{:T(128)}) while((s32[]{:T(128)}, f32[512,512]{1,0:T(8,128)}, s32[4,2]{0,1:T(2,128)S(1)}, f32[4,128,128]{2,1,0:T(8,128)S(1)}, s32[]{:T(128)}) %tuple.33), condition=%wide.while_cond, body=%wide.while_body.sunk | while | flops 2 | bytes 131181 | solution.py:23
  405.1 0.1 constant_dynamic-slice_fusion.2
  405.1 0.6 fusion.41
  405.7 2.2 bitcast_dynamic-update-slice_fusion.2
  408.0 0.1 constant_dynamic-slice_fusion.2
  408.1 0.6 fusion.41
  408.7 2.2 bitcast_dynamic-update-slice_fusion.2
  410.9 0.1 constant_dynamic-slice_fusion.2
  411.0 0.6 fusion.41
  411.6 2.2 bitcast_dynamic-update-slice_fusion.2
  413.9 0.1 constant_dynamic-slice_fusion.2
  414.0 0.6 fusion.41
  414.6 2.2 bitcast_dynamic-update-slice_fusion.2
  416.8 39.3 %custom-call.33 = f32[4,128,128]{1,2,0:T(8,128)S(1)} custom-call(f32[4,128,128]{2,1,0:T(8,128)S(1)} %get-tuple-element.9), custom_call_target="InvertDiagBlocksLowerTriangular" | custom-call | tf_op jit(solution)/shard_map/triangular_solve | solution.py:23
  456.1 0.3 fusion.18
  456.4 1.2 convolution_subtract_fusion.4
  457.6 0.3 fusion.22
  458.0 1.5 convolution_subtract_fusion.2
  459.5 0.3 fusion.21
  459.8 1.8 convolution_subtract_fusion.1
  461.5 0.3 fusion.20
  461.9 1.0 copy.5
  462.9 1.3 copy.6
  (14 shorter events, 0.2 us)
Async XLA Ops:
  7.2 311.3 %all-reduce.3.cloned.1.call-start = ((), (), s32[]{:S(2)}) async-start(), calls=%async_computation | async-start | bytes 2097152 | tf_op jit(solution)/shard_map/psum | solution.py:17
  318.5 1.7 copy-start.1
  403.8 52.3 %copy-start = (f32[256,512]{1,0:T(8,128)S(1)}, f32[256,512]{1,0:T(8,128)}, u32[]{:S(2)}) copy-start(f32[256,512]{1,0:T(8,128)} %param.1) | copy-start | bytes 1572868
Sparse Core Ops, SparseCore 0:
  13.3 305.1 all-reduce.2
where the time goes:
time: 472 us; the launch traced here: 471 us
  waiting for transfers between devices  308 us (65%)
  other arithmetic  120 us (25%)
  between operations  16.8 us (4%)
  local copies, waits for them, and re-layouts  15.7 us (3%)
  matrix products  10.9 us (2%)
    psum x1, waiting for transfers between devices, summed_gram(): return lax.psum(gram, ('rows', 'chip'))  308 us
    another operation x14, other arithmetic, on_device(): lower = jnp.linalg.cholesky(summed_gram(spectra))  78.8 us
    another operation x2, other arithmetic, on_device(): lax.linalg.triangular_solve(lower, spectra, left_side=False, lower=True,...  39.3 us
    another operation x12, local copies, waits for them, and re-layouts  11.6 us
  transfers between devices with their start and end apart: 1, of which 1 were waited for; matrix products, arithmetic and copies ran while one was open for 0% of the time, Pallas kernels for 0%

commit v1 on v0

v1 whole, which is shorter than its diff:
```python
import math

import jax
import jax.numpy as jnp
from jax import lax
from jax.sharding import PartitionSpec as P

AXES = ("rows", "chip")


def local_gram(block):
    return lax.dot_general(
        block,
        block,
        (((0,), (0,)), ((), ())),
        precision=lax.Precision.HIGHEST,
        preferred_element_type=jnp.float32,
    )


def summed(gram):
    n_dev = lax.axis_size("rows") * lax.axis_size("chip")
    steps = int(math.log2(n_dev))
    assert 1 << steps == n_dev
    me = lax.axis_index(AXES)
    shape = gram.shape
    x = gram.reshape(-1, 128)
    masks = [1 << k for k in range(steps)]
    for m in masks:
        half = x.shape[0] // 2
        bit = (me // m) % 2
        keep = lax.dynamic_slice_in_dim(x, bit * half, half, 0)
        send = lax.dynamic_slice_in_dim(x, (1 - bit) * half, half, 0)
        perm = [(i, i ^ m) for i in range(n_dev)]
        x = keep + lax.ppermute(send, AXES, perm)
    for m in reversed(masks):
        bit = (me // m) % 2
        perm = [(i, i ^ m) for i in range(n_dev)]
        other = lax.ppermute(x, AXES, perm)
        lo = jnp.where(bit == 0, x, other)
        hi = jnp.where(bit == 0, other, x)
        x = jnp.concatenate([lo, hi], axis=0)
    return x.reshape(shape)


def on_device(spectra):
    total_rows = lax.axis_size("rows") * lax.axis_size("chip") * spectra.shape[0]
    lower = jnp.linalg.cholesky(summed(local_gram(spectra)))
    basis = lax.linalg.triangular_solve(
        lower, spectra, left_side=False, lower=True, transpose_a=True
    )
    factor_scale = math.sqrt(total_rows)
    return (basis * factor_scale, lower.T / factor_scale)


def solution(mesh):
    return jax.shard_map(
        on_device,
        mesh=mesh,
        in_specs=(P(AXES, None),),
        out_specs=(P(AXES, None), P()),
        check_vma=False,
    )
```

time: 472 us -> 315 us (0.67)
  waiting for transfers between devices: 308 us -> 87.5 us
  starting transfers between devices: 0.04 us -> 77.8 us
  between operations: 16.8 us -> 4.16 us
    psum x1 -> x0, waiting for transfers between devices: 308 us -> none  [summed_gram(): return lax.psum(gram, ('rows', 'chip'))]
    ppermute x0 -> x20, waiting for transfers between devices: none -> 87.5 us  [the longest x10 47.1 us: summed(): x = keep + lax.ppermute(send, AXES, perm)]
    ppermute x0 -> x20, starting transfers between devices: none -> 77.8 us  [the longest x10 41.3 us: summed(): other = lax.ppermute(x, AXES, perm)]
  transfers between devices with their start and end apart: 1 -> 20, of which waited for: 1 -> 20; matrix products, arithmetic and copies ran while one was open for 0% -> 0% of each run, Pallas kernels for 0% -> 0%
where the time goes in v1:
time: 315 us; the launch traced here: 314 us
  other arithmetic  120 us (38%)
  waiting for transfers between devices  87.5 us (28%)
  starting transfers between devices  77.8 us (25%)
  local copies, waits for them, and re-layouts  14.3 us (5%)
  matrix products  9.83 us (3%)
  between operations  4.16 us (1%)
    another operation x14, other arithmetic, on_device(): lower = jnp.linalg.cholesky(summed(local_gram(spectra)))  78.7 us
    ppermute x10, waiting for transfers between devices, summed(): x = keep + lax.ppermute(send, AXES, perm)  47.1 us
    ppermute x10, starting transfers between devices, summed(): other = lax.ppermute(x, AXES, perm)  41.3 us
    ppermute x10, waiting for transfers between devices, summed(): other = lax.ppermute(x, AXES, perm)  40.4 us
    another operation x2, other arithmetic, on_device(): lax.linalg.triangular_solve(lower, spectra, left_side=False, lower=True,...  39.3 us
    ppermute x10, starting transfers between devices, summed(): x = keep + lax.ppermute(send, AXES, perm)  36.5 us
    another operation x12, local copies, waits for them, and re-layouts  11.1 us
  transfers between devices with their start and end apart: 20, of which 20 were waited for; matrix products, arithmetic and copies ran while one was open for 0% of the time, Pallas kernels for 0%

profile of v1, /device:TPU:1, one launch (start us, length us, event | category | flops | bytes accessed | tf_op | source)
XLA Modules:
  0.0 313.7 jit_solution(2744315181107070230)
XLA Ops:
  0.6 2.2 fusion.35
  3.0 16.0 %collective-permute-start = (f32[1024,128]{1,0:T(8,128)S(1)}, f32[1024,128]{1,0:T(8,128)S(1)}, u32[]{:S(2)}, u32[]{:S(2)}) collective-permute-start(f32[1024,128]{1,0:T(8,128)S(1)} %constant_dynamic-slice_fusion.13), channel_id=1, source_target_pairs={{0,1},{1,0},{2,3},{3,2},{4,5},{5,4},{6,7},{7,6},{8,9},{9,8},{10,11... | collective-permute-start | bytes 1572872 | tf_op jit(solution)/shard_map/ppermute | solution.py:35
  20.7 1.9 collective-permute-start.1
  22.6 7.4 %collective-permute-done.1 = f32[512,128]{1,0:T(8,128)S(1)} collective-permute-done((f32[512,128]{1,0:T(8,128)S(1)}, f32[512,128]{1,0:T(8,128)S(1)}, u32[]{:S(2)}, u32[]{:S(2)}) %collective-permute-start.1) | collective-permute-done | bytes 262176 | tf_op jit(solution)/shard_map/ppermute | solution.py:35
  30.1 1.9 collective-permute-start.2
  32.1 9.0 %collective-permute-done.2 = f32[256,128]{1,0:T(8,128)S(1)} collective-permute-done((f32[256,128]{1,0:T(8,128)S(1)}, f32[256,128]{1,0:T(8,128)S(1)}, u32[]{:S(2)}, u32[]{:S(2)}) %collective-permute-start.2) | collective-permute-done | bytes 131104 | tf_op jit(solution)/shard_map/ppermute | solution.py:35
  41.1 3.3 %collective-permute-start.3 = (f32[128,128]{1,0:T(8,128)S(1)}, f32[128,128]{1,0:T(8,128)S(1)}, u32[]{:S(2)}, u32[]{:S(2)}) collective-permute-start(f32[128,128]{1,0:T(8,128)S(1)} %constant_dynamic-slice_fusion.10), channel_id=1, source_target_pairs={{0,8},{1,9},{2,10},{3,11},{4,12},{5,13},{6,14},{7,15},{8,0},{9,1},... | collective-permute-start | bytes 196616 | tf_op jit(solution)/shard_map/ppermute | solution.py:35
  44.5 6.7 %collective-permute-done.3 = f32[128,128]{1,0:T(8,128)S(1)} collective-permute-done((f32[128,128]{1,0:T(8,128)S(1)}, f32[128,128]{1,0:T(8,128)S(1)}, u32[]{:S(2)}, u32[]{:S(2)}) %collective-permute-start.3) | collective-permute-done | bytes 65568 | tf_op jit(solution)/shard_map/ppermute | solution.py:35
  51.2 1.9 collective-permute-start.4
  53.2 2.7 collective-permute-done.4
  55.9 1.9 collective-permute-start.5
  57.8 3.4 %collective-permute-done.5 = f32[32,128]{1,0:T(8,128)S(1)} collective-permute-done((f32[32,128]{1,0:T(8,128)S(1)}, f32[32,128]{1,0:T(8,128)S(1)}, u32[]{:S(2)}, u32[]{:S(2)}) %collective-permute-start.5) | collective-permute-done | bytes 16416 | tf_op jit(solution)/shard_map/ppermute | solution.py:35
  61.3 2.8 collective-permute-start.6
  64.1 5.5 %collective-permute-done.6 = f32[16,128]{1,0:T(8,128)S(1)} collective-permute-done((f32[16,128]{1,0:T(8,128)S(1)}, f32[16,128]{1,0:T(8,128)S(1)}, u32[]{:S(2)}, u32[]{:S(2)}) %collective-permute-start.6) | collective-permute-done | bytes 8224 | tf_op jit(solution)/shard_map/ppermute | solution.py:35
  71.5 2.4 collective-permute-done.7
  75.9 3.3 %collective-permute-done.8 = f32[4,128]{1,0:T(4,128)S(1)} collective-permute-done((f32[4,128]{1,0:T(4,128)S(1)}, f32[4,128]{1,0:T(4,128)S(1)}, u32[]{:S(2)}, u32[]{:S(2)}) %collective-permute-start.8) | collective-permute-done | bytes 2080 | tf_op jit(solution)/shard_map/ppermute | solution.py:35
  79.2 2.9 collective-permute-start.9
  82.1 5.3 %collective-permute-done.9 = f32[2,128]{1,0:T(2,128)S(1)} collective-permute-done((f32[2,128]{1,0:T(2,128)S(1)}, f32[2,128]{1,0:T(2,128)S(1)}, u32[]{:S(2)}, u32[]{:S(2)}) %collective-permute-start.9) | collective-permute-done | bytes 1056 | tf_op jit(solution)/shard_map/ppermute | solution.py:35
  87.4 2.9 collective-permute-start.10
  90.3 5.3 %collective-permute-done.10 = f32[2,128]{1,0:T(2,128)S(1)} collective-permute-done((f32[2,128]{1,0:T(2,128)S(1)}, f32[2,128]{1,0:T(2,128)S(1)}, u32[]{:S(2)}, u32[]{:S(2)}) %collective-permute-start.10) | collective-permute-done | bytes 1056 | tf_op jit(solution)/shard_map/ppermute | solution.py:39
  97.6 3.3 %collective-permute-done.11 = f32[4,128]{1,0:T(4,128)S(1)} collective-permute-done((f32[4,128]{1,0:T(4,128)S(1)}, f32[4,128]{1,0:T(4,128)S(1)}, u32[]{:S(2)}, u32[]{:S(2)}) %collective-permute-start.11) | collective-permute-done | bytes 2080 | tf_op jit(solution)/shard_map/ppermute | solution.py:39
  100.9 1.9 collective-permute-start.12
  102.8 2.4 collective-permute-done.12
  105.3 3.4 %collective-permute-start.13 = (f32[16,128]{1,0:T(8,128)S(1)}, f32[16,128]{1,0:T(8,128)S(1)}, u32[]{:S(2)}, u32[]{:S(2)}) collective-permute-start(f32[16,128]{1,0:T(8,128)S(1)} %pad_maximum_fusion.7), channel_id=1, source_target_pairs={{0,64},{1,65},{2,66},{3,67},{4,68},{5,69},{6,70},{7,71},{8,72},{9,... | collective-permute-start | bytes 24584 | tf_op jit(solution)/shard_map/ppermute | solution.py:39
  108.6 4.9 %collective-permute-done.13 = f32[16,128]{1,0:T(8,128)S(1)} collective-permute-done((f32[16,128]{1,0:T(8,128)S(1)}, f32[16,128]{1,0:T(8,128)S(1)}, u32[]{:S(2)}, u32[]{:S(2)}) %collective-permute-start.13) | collective-permute-done | bytes 8224 | tf_op jit(solution)/shard_map/ppermute | solution.py:39
  115.5 3.4 %collective-permute-done.14 = f32[32,128]{1,0:T(8,128)S(1)} collective-permute-done((f32[32,128]{1,0:T(8,128)S(1)}, f32[32,128]{1,0:T(8,128)S(1)}, u32[]{:S(2)}, u32[]{:S(2)}) %collective-permute-start.14) | collective-permute-done | bytes 16416 | tf_op jit(solution)/shard_map/ppermute | solution.py:39
  119.0 1.9 collective-permute-start.15
  120.9 3.0 collective-permute-done.15
  123.9 3.1 %collective-permute-start.16 = (f32[128,128]{1,0:T(8,128)S(1)}, f32[128,128]{1,0:T(8,128)S(1)}, u32[]{:S(2)}, u32[]{:S(2)}) collective-permute-start(f32[128,128]{1,0:T(8,128)S(1)} %pad_maximum_fusion.4), channel_id=1, source_target_pairs={{0,8},{1,9},{2,10},{3,11},{4,12},{5,13},{6,14},{7,15},{8,0},{9,1},... | collective-permute-start | bytes 196616 | tf_op jit(solution)/shard_map/ppermute | solution.py:39
  127.1 5.8 %collective-permute-done.16 = f32[128,128]{1,0:T(8,128)S(1)} collective-permute-done((f32[128,128]{1,0:T(8,128)S(1)}, f32[128,128]{1,0:T(8,128)S(1)}, u32[]{:S(2)}, u32[]{:S(2)}) %collective-permute-start.16) | collective-permute-done | bytes 65568 | tf_op jit(solution)/shard_map/ppermute | solution.py:39
  132.9 1.9 collective-permute-start.17
  134.8 4.7 %collective-permute-done.17 = f32[256,128]{1,0:T(8,128)S(1)} collective-permute-done((f32[256,128]{1,0:T(8,128)S(1)}, f32[256,128]{1,0:T(8,128)S(1)}, u32[]{:S(2)}, u32[]{:S(2)}) %collective-permute-start.17) | collective-permute-done | bytes 131104 | tf_op jit(solution)/shard_map/ppermute | solution.py:39
  139.5 1.9 collective-permute-start.18
  141.5 6.3 %collective-permute-done.18 = f32[512,128]{1,0:T(8,128)S(1)} collective-permute-done((f32[512,128]{1,0:T(8,128)S(1)}, f32[512,128]{1,0:T(8,128)S(1)}, u32[]{:S(2)}, u32[]{:S(2)}) %collective-permute-start.18) | collective-permute-done | bytes 262176 | tf_op jit(solution)/shard_map/ppermute | solution.py:39
  147.8 20.3 %collective-permute-start.19 = (f32[1024,128]{1,0:T(8,128)S(1)}, f32[1024,128]{1,0:T(8,128)S(1)}, u32[]{:S(2)}, u32[]{:S(2)}) collective-permute-start(f32[1024,128]{1,0:T(8,128)S(1)} %pad_maximum_fusion.1), channel_id=1, source_target_pairs={{0,1},{1,0},{2,3},{3,2},{4,5},{5,4},{6,7},{7,6},{8,9},{9,8},{10,11... | collective-permute-start | bytes 1572872 | tf_op jit(solution)/shard_map/ppermute | solution.py:39
  170.4 11.7 %cholesky.104 = f32[128,128]{1,0:T(8,128)S(1)} custom-call(f32[128,128]{1,0:T(8,128)S(1)} %cholesky.266), custom_call_target="Cholesky" | custom-call | tf_op jit(solution)/shard_map/jit(cholesky)/cholesky | solution.py:48
  182.3 9.8 %custom-call.30 = f32[1,128,128]{1,2,0:T(8,128)S(1)} custom-call(f32[1,128,128]{2,1,0:T(8,128)S(1)} %get-tuple-element.43), custom_call_target="InvertDiagBlocksLowerTriangular" | custom-call | tf_op jit(solution)/shard_map/jit(cholesky)/cholesky | solution.py:48
  192.8 11.7 %cholesky.217 = f32[128,128]{1,0:T(8,128)S(1)} custom-call(f32[128,128]{1,0:T(8,128)S(1)} %cholesky.270), custom_call_target="Cholesky" | custom-call | tf_op jit(solution)/shard_map/jit(cholesky)/cholesky | solution.py:48
  204.5 10.0 %custom-call.31 = f32[1,128,128]{1,2,0:T(8,128)S(1)} custom-call(f32[1,128,128]{2,1,0:T(8,128)S(1)} %get-tuple-element.40), custom_call_target="InvertDiagBlocksLowerTriangular" | custom-call | tf_op jit(solution)/shard_map/jit(cholesky)/cholesky | solution.py:48
  215.2 11.7 %cholesky.238 = f32[128,128]{1,0:T(8,128)S(1)} custom-call(f32[128,128]{1,0:T(8,128)S(1)} %cholesky.275), custom_call_target="Cholesky" | custom-call | tf_op jit(solution)/shard_map/jit(cholesky)/cholesky | solution.py:48
  227.6 9.8 %custom-call.32 = f32[1,128,128]{1,2,0:T(8,128)S(1)} custom-call(f32[1,128,128]{2,1,0:T(8,128)S(1)} %get-tuple-element.37), custom_call_target="InvertDiagBlocksLowerTriangular" | custom-call | tf_op jit(solution)/shard_map/jit(cholesky)/cholesky | solution.py:48
  238.0 11.9 %cholesky.255 = f32[128,128]{1,0:T(8,128)S(1)} custom-call(f32[128,128]{1,0:T(8,128)S(1)} %convolution_subtract_fusion.5), custom_call_target="Cholesky" | custom-call | tf_op jit(solution)/shard_map/jit(cholesky)/cholesky | solution.py:48
  255.0 11.2 %while.1 = (s32[]{:T(128)}, f32[512,512]{1,0:T(8,128)}, s32[4,2]{0,1:T(2,128)S(1)}, f32[4,128,128]{2,1,0:T(8,128)S(1)}, s32[]{:T(128)}) while((s32[]{:T(128)}, f32[512,512]{1,0:T(8,128)}, s32[4,2]{0,1:T(2,128)S(1)}, f32[4,128,128]{2,1,0:T(8,128)S(1)}, s32[]{:T(128)}) %tuple.44), condition=%wide.while_cond, body=%wide.while_body.sunk | while | flops 2 | bytes 131181 | solution.py:49
  255.7 2.2 bitcast_dynamic-update-slice_fusion.2
  258.5 2.2 bitcast_dynamic-update-slice_fusion.2
  261.3 2.2 bitcast_dynamic-update-slice_fusion.2
  264.1 2.1 bitcast_dynamic-update-slice_fusion.2
  266.2 39.3 %custom-call.33 = f32[4,128,128]{1,2,0:T(8,128)S(1)} custom-call(f32[4,128,128]{2,1,0:T(8,128)S(1)} %get-tuple-element.9), custom_call_target="InvertDiagBlocksLowerTriangular" | custom-call | tf_op jit(solution)/shard_map/triangular_solve | solution.py:49
  (91 shorter events, 27.8 us)
Async XLA Ops:
  3.0 17.5 %collective-permute-start = (f32[1024,128]{1,0:T(8,128)S(1)}, f32[1024,128]{1,0:T(8,128)S(1)}, u32[]{:S(2)}, u32[]{:S(2)}) collective-permute-start(f32[1024,128]{1,0:T(8,128)S(1)} %constant_dynamic-slice_fusion.13), channel_id=1, source_target_pairs={{0,1},{1,0},{2,3},{3,2},{4,5},{5,4},{6,7},{7,6},{8,9},{9,8},{10,11... | collective-permute-start | bytes 1572872 | tf_op jit(solution)/shard_map/ppermute | solution.py:35
  20.7 9.4 %collective-permute-start.1 = (f32[512,128]{1,0:T(8,128)S(1)}, f32[512,128]{1,0:T(8,128)S(1)}, u32[]{:S(2)}, u32[]{:S(2)}) collective-permute-start(f32[512,128]{1,0:T(8,128)S(1)} %constant_dynamic-slice_fusion.12), channel_id=1, source_target_pairs={{0,2},{1,3},{2,0},{3,1},{4,6},{5,7},{6,4},{7,5},{8,10},{9,11},{10,... | collective-permute-start | bytes 786440 | tf_op jit(solution)/shard_map/ppermute | solution.py:35
  30.1 11.0 %collective-permute-start.2 = (f32[256,128]{1,0:T(8,128)S(1)}, f32[256,128]{1,0:T(8,128)S(1)}, u32[]{:S(2)}, u32[]{:S(2)}) collective-permute-start(f32[256,128]{1,0:T(8,128)S(1)} %constant_dynamic-slice_fusion.11), channel_id=1, source_target_pairs={{0,4},{1,5},{2,6},{3,7},{4,0},{5,1},{6,2},{7,3},{8,12},{9,13},{10,... | collective-permute-start | bytes 393224 | tf_op jit(solution)/shard_map/ppermute | solution.py:35
  41.1 10.0 %collective-permute-start.3 = (f32[128,128]{1,0:T(8,128)S(1)}, f32[128,128]{1,0:T(8,128)S(1)}, u32[]{:S(2)}, u32[]{:S(2)}) collective-permute-start(f32[128,128]{1,0:T(8,128)S(1)} %constant_dynamic-slice_fusion.10), channel_id=1, source_target_pairs={{0,8},{1,9},{2,10},{3,11},{4,12},{5,13},{6,14},{7,15},{8,0},{9,1},... | collective-permute-start | bytes 196616 | tf_op jit(solution)/shard_map/ppermute | solution.py:35
  51.2 4.7 %collective-permute-start.4 = (f32[64,128]{1,0:T(8,128)S(1)}, f32[64,128]{1,0:T(8,128)S(1)}, u32[]{:S(2)}, u32[]{:S(2)}) collective-permute-start(f32[64,128]{1,0:T(8,128)S(1)} %constant_dynamic-slice_fusion.9), channel_id=1, source_target_pairs={{0,16},{1,17},{2,18},{3,19},{4,20},{5,21},{6,22},{7,23},{8,24},{9,... | collective-permute-start | bytes 98312 | tf_op jit(solution)/shard_map/ppermute | solution.py:35
  55.9 5.4 %collective-permute-start.5 = (f32[32,128]{1,0:T(8,128)S(1)}, f32[32,128]{1,0:T(8,128)S(1)}, u32[]{:S(2)}, u32[]{:S(2)}) collective-permute-start(f32[32,128]{1,0:T(8,128)S(1)} %constant_dynamic-slice_fusion.8), channel_id=1, source_target_pairs={{0,32},{1,33},{2,34},{3,35},{4,36},{5,37},{6,38},{7,39},{8,40},{9,... | collective-permute-start | bytes 49160 | tf_op jit(solution)/shard_map/ppermute | solution.py:35
  61.3 8.3 %collective-permute-start.6 = (f32[16,128]{1,0:T(8,128)S(1)}, f32[16,128]{1,0:T(8,128)S(1)}, u32[]{:S(2)}, u32[]{:S(2)}) collective-permute-start(f32[16,128]{1,0:T(8,128)S(1)} %constant_dynamic-slice_fusion.7), channel_id=1, source_target_pairs={{0,64},{1,65},{2,66},{3,67},{4,68},{5,69},{6,70},{7,71},{8,72},{9,... | collective-permute-start | bytes 24584 | tf_op jit(solution)/shard_map/ppermute | solution.py:35
  69.6 4.3 %collective-permute-start.7 = (f32[8,128]{1,0:T(8,128)S(1)}, f32[8,128]{1,0:T(8,128)S(1)}, u32[]{:S(2)}, u32[]{:S(2)}) collective-permute-start(f32[8,128]{1,0:T(8,128)S(1)} %constant_dynamic-slice_fusion.5), channel_id=1, source_target_pairs={{0,128},{1,129},{2,130},{3,131},{4,132},{5,133},{6,134},{7,135},{8... | collective-permute-start | bytes 12296 | tf_op jit(solution)/shard_map/ppermute | solution.py:35
  73.9 5.2 %collective-permute-start.8 = (f32[4,128]{1,0:T(4,128)S(1)}, f32[4,128]{1,0:T(4,128)S(1)}, u32[]{:S(2)}, u32[]{:S(2)}) collective-permute-start(f32[4,128]{1,0:T(4,128)S(1)} %constant_dynamic-slice_fusion.3), channel_id=1, source_target_pairs={{0,256},{1,257},{2,258},{3,259},{4,260},{5,261},{6,262},{7,263},{8... | collective-permute-start | bytes 6152 | tf_op jit(solution)/shard_map/ppermute | solution.py:35
  79.2 8.2 %collective-permute-start.9 = (f32[2,128]{1,0:T(2,128)S(1)}, f32[2,128]{1,0:T(2,128)S(1)}, u32[]{:S(2)}, u32[]{:S(2)}) collective-permute-start(f32[2,128]{1,0:T(2,128)S(1)} %constant_dynamic-slice_fusion.1), channel_id=1, source_target_pairs={{0,512},{1,513},{2,514},{3,515},{4,516},{5,517},{6,518},{7,519},{8... | collective-permute-start | bytes 3080 | tf_op jit(solution)/shard_map/ppermute | solution.py:35
  87.4 8.2 %collective-permute-start.10 = (f32[2,128]{1,0:T(2,128)S(1)}, f32[2,128]{1,0:T(2,128)S(1)}, u32[]{:S(2)}, u32[]{:S(2)}) collective-permute-start(f32[2,128]{1,0:T(2,128)S(1)} %fusion.31), channel_id=1, source_target_pairs={{0,512},{1,513},{2,514},{3,515},{4,516},{5,517},{6,518},{7,519},{8... | collective-permute-start | bytes 3080 | tf_op jit(solution)/shard_map/ppermute | solution.py:39
  95.6 5.2 %collective-permute-start.11 = (f32[4,128]{1,0:T(4,128)S(1)}, f32[4,128]{1,0:T(4,128)S(1)}, u32[]{:S(2)}, u32[]{:S(2)}) collective-permute-start(f32[4,128]{1,0:T(4,128)S(1)} %pad_maximum_fusion.9), channel_id=1, source_target_pairs={{0,256},{1,257},{2,258},{3,259},{4,260},{5,261},{6,262},{7,263},{8... | collective-permute-start | bytes 6152 | tf_op jit(solution)/shard_map/ppermute | solution.py:39
  100.9 4.4 %collective-permute-start.12 = (f32[8,128]{1,0:T(8,128)S(1)}, f32[8,128]{1,0:T(8,128)S(1)}, u32[]{:S(2)}, u32[]{:S(2)}) collective-permute-start(f32[8,128]{1,0:T(8,128)S(1)} %pad_maximum_fusion.8), channel_id=1, source_target_pairs={{0,128},{1,129},{2,130},{3,131},{4,132},{5,133},{6,134},{7,135},{8... | collective-permute-start | bytes 12296 | tf_op jit(solution)/shard_map/ppermute | solution.py:39
  105.3 8.3 %collective-permute-start.13 = (f32[16,128]{1,0:T(8,128)S(1)}, f32[16,128]{1,0:T(8,128)S(1)}, u32[]{:S(2)}, u32[]{:S(2)}) collective-permute-start(f32[16,128]{1,0:T(8,128)S(1)} %pad_maximum_fusion.7), channel_id=1, source_target_pairs={{0,64},{1,65},{2,66},{3,67},{4,68},{5,69},{6,70},{7,71},{8,72},{9,... | collective-permute-start | bytes 24584 | tf_op jit(solution)/shard_map/ppermute | solution.py:39
  113.6 5.4 %collective-permute-start.14 = (f32[32,128]{1,0:T(8,128)S(1)}, f32[32,128]{1,0:T(8,128)S(1)}, u32[]{:S(2)}, u32[]{:S(2)}) collective-permute-start(f32[32,128]{1,0:T(8,128)S(1)} %pad_maximum_fusion.6), channel_id=1, source_target_pairs={{0,32},{1,33},{2,34},{3,35},{4,36},{5,37},{6,38},{7,39},{8,40},{9,... | collective-permute-start | bytes 49160 | tf_op jit(solution)/shard_map/ppermute | solution.py:39
  119.0 5.0 %collective-permute-start.15 = (f32[64,128]{1,0:T(8,128)S(1)}, f32[64,128]{1,0:T(8,128)S(1)}, u32[]{:S(2)}, u32[]{:S(2)}) collective-permute-start(f32[64,128]{1,0:T(8,128)S(1)} %pad_maximum_fusion.5), channel_id=1, source_target_pairs={{0,16},{1,17},{2,18},{3,19},{4,20},{5,21},{6,22},{7,23},{8,24},{9,... | collective-permute-start | bytes 98312 | tf_op jit(solution)/shard_map/ppermute | solution.py:39
  123.9 8.9 %collective-permute-start.16 = (f32[128,128]{1,0:T(8,128)S(1)}, f32[128,128]{1,0:T(8,128)S(1)}, u32[]{:S(2)}, u32[]{:S(2)}) collective-permute-start(f32[128,128]{1,0:T(8,128)S(1)} %pad_maximum_fusion.4), channel_id=1, source_target_pairs={{0,8},{1,9},{2,10},{3,11},{4,12},{5,13},{6,14},{7,15},{8,0},{9,1},... | collective-permute-start | bytes 196616 | tf_op jit(solution)/shard_map/ppermute | solution.py:39
  132.9 6.6 %collective-permute-start.17 = (f32[256,128]{1,0:T(8,128)S(1)}, f32[256,128]{1,0:T(8,128)S(1)}, u32[]{:S(2)}, u32[]{:S(2)}) collective-permute-start(f32[256,128]{1,0:T(8,128)S(1)} %pad_maximum_fusion.3), channel_id=1, source_target_pairs={{0,4},{1,5},{2,6},{3,7},{4,0},{5,1},{6,2},{7,3},{8,12},{9,13},{10,... | collective-permute-start | bytes 393224 | tf_op jit(solution)/shard_map/ppermute | solution.py:39
  139.5 8.2 %collective-permute-start.18 = (f32[512,128]{1,0:T(8,128)S(1)}, f32[512,128]{1,0:T(8,128)S(1)}, u32[]{:S(2)}, u32[]{:S(2)}) collective-permute-start(f32[512,128]{1,0:T(8,128)S(1)} %pad_maximum_fusion.2), channel_id=1, source_target_pairs={{0,2},{1,3},{2,0},{3,1},{4,6},{5,7},{6,4},{7,5},{8,10},{9,11},{10,... | collective-permute-start | bytes 786440 | tf_op jit(solution)/shard_map/ppermute | solution.py:39
  147.8 21.7 %collective-permute-start.19 = (f32[1024,128]{1,0:T(8,128)S(1)}, f32[1024,128]{1,0:T(8,128)S(1)}, u32[]{:S(2)}, u32[]{:S(2)}) collective-permute-start(f32[1024,128]{1,0:T(8,128)S(1)} %pad_maximum_fusion.1), channel_id=1, source_target_pairs={{0,1},{1,0},{2,3},{3,2},{4,5},{5,4},{6,7},{7,6},{8,9},{9,8},{10,11... | collective-permute-start | bytes 1572872 | tf_op jit(solution)/shard_map/ppermute | solution.py:39
  253.8 51.8 %copy-start = (f32[256,512]{1,0:T(8,128)S(1)}, f32[256,512]{1,0:T(8,128)}, u32[]{:S(2)}) copy-start(f32[256,512]{1,0:T(8,128)} %param.1) | copy-start | bytes 1572868

commit v2 on v1

--- a/solution.py
+++ b/solution.py
@@ -6,15 +6,12 @@
 from jax.sharding import PartitionSpec as P
 
 AXES = ("rows", "chip")
+BLOCK = 128
 
 
-def local_gram(block):
+def mm(a, b, dims):
     return lax.dot_general(
-        block,
-        block,
-        (((0,), (0,)), ((), ())),
-        precision=lax.Precision.HIGHEST,
-        preferred_element_type=jnp.float32,
+        a, b, (dims, ((), ())), precision=lax.Precision.HIGHEST, preferred_element_type=jnp.float32
     )
 
 
@@ -43,12 +40,49 @@
     return x.reshape(shape)
 
 
+def factor(gram):
+    a = (gram + gram.T) / 2
+    n = a.shape[0]
+    nb = n // BLOCK
+    cols, invs = [], []
+    for j in range(nb):
+        s = slice(j * BLOCK, (j + 1) * BLOCK)
+        rest = a[j * BLOCK:, s]
+        if j:
+            done = jnp.concatenate([c[j * BLOCK - k * BLOCK:] for k, c in enumerate(cols)], axis=1)
+            rest = rest - mm(done, done[:BLOCK], ((1,), (1,)))
+        diag = lax.linalg.cholesky(rest[:BLOCK], symmetrize_input=False)
+        inv = lax.linalg.triangular_solve(
+            diag, jnp.eye(BLOCK, dtype=diag.dtype), left_side=True, lower=True
+        )
+        col = diag
+        if j < nb - 1:
+            col = jnp.concatenate([diag, mm(rest[BLOCK:], inv, ((1,), (1,)))], axis=0)
+        cols.append(col)
+        invs.append(inv)
+    lower = jnp.concatenate(
+        [jnp.concatenate([jnp.zeros((k * BLOCK, BLOCK), a.dtype), c], axis=0) for k, c in enumerate(cols)],
+        axis=1,
+    )
+    return lower, invs
+
+
+def whiten(spectra, lower, invs):
+    outs = []
+    for j, inv in enumerate(invs):
+        rhs = spectra[:, j * BLOCK:(j + 1) * BLOCK]
+        if j:
+            prev = jnp.concatenate(outs, axis=1)
+            rhs = rhs - mm(prev, lower[j * BLOCK:(j + 1) * BLOCK, : j * BLOCK], ((1,), (1,)))
+        outs.append(mm(rhs, inv, ((1,), (1,))))
+    return jnp.concatenate(outs, axis=1)
+
+
 def on_device(spectra):
     total_rows = lax.axis_size("rows") * lax.axis_size("chip") * spectra.shape[0]
-    lower = jnp.linalg.cholesky(summed(local_gram(spectra)))
-    basis = lax.linalg.triangular_solve(
-        lower, spectra, left_side=False, lower=True, transpose_a=True
-    )
+    gram = summed(mm(spectra, spectra, ((0,), (0,))))
+    lower, invs = factor(gram)
+    basis = whiten(spectra, lower, invs)
     factor_scale = math.sqrt(total_rows)
     return (basis * factor_scale, lower.T / factor_scale)
 

time: 315 us -> 274 us (0.87)
  other arithmetic: 120 us -> 92.7 us
  local copies, waits for them, and re-layouts: 14.3 us -> 4.74 us
    another operation x16 -> x20, other arithmetic: 118 us -> 91.9 us  [the longest x12 49.9 us: factor(): diag = lax.linalg.cholesky(rest[:BLOCK], symmetrize_input=False)]
    another operation x17 -> x1, local copies, waits for them, and re-layouts: 11.3 us -> 0.01 us  [factor(): diag = lax.linalg.cholesky(rest[:BLOCK], symmetrize_input=False)]
    another operation x13 -> x4, matrix products: 7.6 us -> 1.14 us  [factor(): lax.linalg.triangular_solve(diag, jnp.eye(BLOCK, dtype=diag.dtype), left_...]
    dot_general x1 -> x14, matrix products: 2.22 us -> 7.64 us  [mm(): lax.dot_general(a, b, (dims, ((), ())), precision=lax.Precision.HIGHEST,...]
where the time goes in v2:
time: 274 us; the launch traced here: 273 us
  other arithmetic  92.7 us (34%)
  waiting for transfers between devices  87.5 us (32%)
  starting transfers between devices  77.8 us (28%)
  matrix products  8.77 us (3%)
  local copies, waits for them, and re-layouts  4.74 us (2%)
    another operation x12, other arithmetic, factor(): diag = lax.linalg.cholesky(rest[:BLOCK], symmetrize_input=False)  49.9 us
    ppermute x10, waiting for transfers between devices, summed(): x = keep + lax.ppermute(send, AXES, perm)  47.1 us
    another operation x8, other arithmetic, factor(): lax.linalg.triangular_solve(diag, jnp.eye(BLOCK, dtype=diag.dtype), left_...  42 us
    ppermute x10, starting transfers between devices, summed(): other = lax.ppermute(x, AXES, perm)  41.3 us
    ppermute x10, waiting for transfers between devices, summed(): other = lax.ppermute(x, AXES, perm)  40.4 us
    ppermute x10, starting transfers between devices, summed(): x = keep + lax.ppermute(send, AXES, perm)  36.5 us
    dot_general x14, matrix products, mm(): lax.dot_general(a, b, (dims, ((), ())), precision=lax.Precision.HIGHEST,...  7.64 us
  transfers between devices with their start and end apart: 20, of which 20 were waited for; matrix products, arithmetic and copies ran while one was open for 0% of the time, Pallas kernels for 0%

profile of v2, /device:TPU:1, one launch (start us, length us, event | category | flops | bytes accessed | tf_op | source)
XLA Modules:
  0.0 273.4 jit_solution(10337217864998316185)
XLA Ops:
  0.6 2.2 fusion.64
  3.0 16.0 %collective-permute-start = (f32[1024,128]{1,0:T(8,128)S(1)}, f32[1024,128]{1,0:T(8,128)S(1)}, u32[]{:S(2)}, u32[]{:S(2)}) collective-permute-start(f32[1024,128]{1,0:T(8,128)S(1)} %constant_dynamic-slice_fusion.12), channel_id=1, source_target_pairs={{0,1},{1,0},{2,3},{3,2},{4,5},{5,4},{6,7},{7,6},{8,9},{9,8},{10,11... | collective-permute-start | bytes 1572872 | tf_op jit(solution)/shard_map/ppermute | solution.py:32
  19.1 1.5 collective-permute-done
  20.7 1.9 collective-permute-start.1
  22.6 7.4 %collective-permute-done.1 = f32[512,128]{1,0:T(8,128)S(1)} collective-permute-done((f32[512,128]{1,0:T(8,128)S(1)}, f32[512,128]{1,0:T(8,128)S(1)}, u32[]{:S(2)}, u32[]{:S(2)}) %collective-permute-start.1) | collective-permute-done | bytes 262176 | tf_op jit(solution)/shard_map/ppermute | solution.py:32
  30.1 1.9 collective-permute-start.2
  32.1 9.0 %collective-permute-done.2 = f32[256,128]{1,0:T(8,128)S(1)} collective-permute-done((f32[256,128]{1,0:T(8,128)S(1)}, f32[256,128]{1,0:T(8,128)S(1)}, u32[]{:S(2)}, u32[]{:S(2)}) %collective-permute-start.2) | collective-permute-done | bytes 131104 | tf_op jit(solution)/shard_map/ppermute | solution.py:32
  41.1 3.3 %collective-permute-start.3 = (f32[128,128]{1,0:T(8,128)S(1)}, f32[128,128]{1,0:T(8,128)S(1)}, u32[]{:S(2)}, u32[]{:S(2)}) collective-permute-start(f32[128,128]{1,0:T(8,128)S(1)} %constant_dynamic-slice_fusion.9), channel_id=1, source_target_pairs={{0,8},{1,9},{2,10},{3,11},{4,12},{5,13},{6,14},{7,15},{8,0},{9,1},... | collective-permute-start | bytes 196616 | tf_op jit(solution)/shard_map/ppermute | solution.py:32
  44.5 6.7 %collective-permute-done.3 = f32[128,128]{1,0:T(8,128)S(1)} collective-permute-done((f32[128,128]{1,0:T(8,128)S(1)}, f32[128,128]{1,0:T(8,128)S(1)}, u32[]{:S(2)}, u32[]{:S(2)}) %collective-permute-start.3) | collective-permute-done | bytes 65568 | tf_op jit(solution)/shard_map/ppermute | solution.py:32
  51.2 1.9 collective-permute-start.4
  53.2 2.7 collective-permute-done.4
  55.9 1.9 collective-permute-start.5
  57.8 3.4 %collective-permute-done.5 = f32[32,128]{1,0:T(8,128)S(1)} collective-permute-done((f32[32,128]{1,0:T(8,128)S(1)}, f32[32,128]{1,0:T(8,128)S(1)}, u32[]{:S(2)}, u32[]{:S(2)}) %collective-permute-start.5) | collective-permute-done | bytes 16416 | tf_op jit(solution)/shard_map/ppermute | solution.py:32
  61.3 2.8 %collective-permute-start.6 = (f32[16,128]{1,0:T(8,128)S(1)}, f32[16,128]{1,0:T(8,128)S(1)}, u32[]{:S(2)}, u32[]{:S(2)}) collective-permute-start(f32[16,128]{1,0:T(8,128)S(1)} %constant_dynamic-slice_fusion.6), channel_id=1, source_target_pairs={{0,64},{1,65},{2,66},{3,67},{4,68},{5,69},{6,70},{7,71},{8,72},{9,... | collective-permute-start | bytes 24584 | tf_op jit(solution)/shard_map/ppermute | solution.py:32
  64.1 5.4 %collective-permute-done.6 = f32[16,128]{1,0:T(8,128)S(1)} collective-permute-done((f32[16,128]{1,0:T(8,128)S(1)}, f32[16,128]{1,0:T(8,128)S(1)}, u32[]{:S(2)}, u32[]{:S(2)}) %collective-permute-start.6) | collective-permute-done | bytes 8224 | tf_op jit(solution)/shard_map/ppermute | solution.py:32
  69.6 1.9 collective-permute-start.7
  71.5 2.4 collective-permute-done.7
  73.9 1.9 collective-permute-start.8
  75.9 3.3 %collective-permute-done.8 = f32[4,128]{1,0:T(4,128)S(1)} collective-permute-done((f32[4,128]{1,0:T(4,128)S(1)}, f32[4,128]{1,0:T(4,128)S(1)}, u32[]{:S(2)}, u32[]{:S(2)}) %collective-permute-start.8) | collective-permute-done | bytes 2080 | tf_op jit(solution)/shard_map/ppermute | solution.py:32
  79.2 2.9 %collective-permute-start.9 = (f32[2,128]{1,0:T(2,128)S(1)}, f32[2,128]{1,0:T(2,128)S(1)}, u32[]{:S(2)}, u32[]{:S(2)}) collective-permute-start(f32[2,128]{1,0:T(2,128)S(1)} %constant_dynamic-slice_fusion), channel_id=1, source_target_pairs={{0,512},{1,513},{2,514},{3,515},{4,516},{5,517},{6,518},{7,519},{8... | collective-permute-start | bytes 3080 | tf_op jit(solution)/shard_map/ppermute | solution.py:32
  82.1 5.3 %collective-permute-done.9 = f32[2,128]{1,0:T(2,128)S(1)} collective-permute-done((f32[2,128]{1,0:T(2,128)S(1)}, f32[2,128]{1,0:T(2,128)S(1)}, u32[]{:S(2)}, u32[]{:S(2)}) %collective-permute-start.9) | collective-permute-done | bytes 1056 | tf_op jit(solution)/shard_map/ppermute | solution.py:32
  87.4 2.9 %collective-permute-start.10 = (f32[2,128]{1,0:T(2,128)S(1)}, f32[2,128]{1,0:T(2,128)S(1)}, u32[]{:S(2)}, u32[]{:S(2)}) collective-permute-start(f32[2,128]{1,0:T(2,128)S(1)} %fusion.58), channel_id=1, source_target_pairs={{0,512},{1,513},{2,514},{3,515},{4,516},{5,517},{6,518},{7,519},{8... | collective-permute-start | bytes 3080 | tf_op jit(solution)/shard_map/ppermute | solution.py:36
  90.3 5.3 %collective-permute-done.10 = f32[2,128]{1,0:T(2,128)S(1)} collective-permute-done((f32[2,128]{1,0:T(2,128)S(1)}, f32[2,128]{1,0:T(2,128)S(1)}, u32[]{:S(2)}, u32[]{:S(2)}) %collective-permute-start.10) | collective-permute-done | bytes 1056 | tf_op jit(solution)/shard_map/ppermute | solution.py:36
  95.6 1.9 collective-permute-start.11
  97.6 3.3 %collective-permute-done.11 = f32[4,128]{1,0:T(4,128)S(1)} collective-permute-done((f32[4,128]{1,0:T(4,128)S(1)}, f32[4,128]{1,0:T(4,128)S(1)}, u32[]{:S(2)}, u32[]{:S(2)}) %collective-permute-start.11) | collective-permute-done | bytes 2080 | tf_op jit(solution)/shard_map/ppermute | solution.py:36
  100.9 1.9 collective-permute-start.12
  102.8 2.4 collective-permute-done.12
  105.3 3.4 %collective-permute-start.13 = (f32[16,128]{1,0:T(8,128)S(1)}, f32[16,128]{1,0:T(8,128)S(1)}, u32[]{:S(2)}, u32[]{:S(2)}) collective-permute-start(f32[16,128]{1,0:T(8,128)S(1)} %pad_maximum_fusion.20), channel_id=1, source_target_pairs={{0,64},{1,65},{2,66},{3,67},{4,68},{5,69},{6,70},{7,71},{8,72},{9,... | collective-permute-start | bytes 24584 | tf_op jit(solution)/shard_map/ppermute | solution.py:36
  108.6 4.9 %collective-permute-done.13 = f32[16,128]{1,0:T(8,128)S(1)} collective-permute-done((f32[16,128]{1,0:T(8,128)S(1)}, f32[16,128]{1,0:T(8,128)S(1)}, u32[]{:S(2)}, u32[]{:S(2)}) %collective-permute-start.13) | collective-permute-done | bytes 8224 | tf_op jit(solution)/shard_map/ppermute | solution.py:36
  113.6 1.9 collective-permute-start.14
  115.5 3.4 %collective-permute-done.14 = f32[32,128]{1,0:T(8,128)S(1)} collective-permute-done((f32[32,128]{1,0:T(8,128)S(1)}, f32[32,128]{1,0:T(8,128)S(1)}, u32[]{:S(2)}, u32[]{:S(2)}) %collective-permute-start.14) | collective-permute-done | bytes 16416 | tf_op jit(solution)/shard_map/ppermute | solution.py:36
  119.0 1.9 collective-permute-start.15
  120.9 3.0 %collective-permute-done.15 = f32[64,128]{1,0:T(8,128)S(1)} collective-permute-done((f32[64,128]{1,0:T(8,128)S(1)}, f32[64,128]{1,0:T(8,128)S(1)}, u32[]{:S(2)}, u32[]{:S(2)}) %collective-permute-start.15) | collective-permute-done | bytes 32800 | tf_op jit(solution)/shard_map/ppermute | solution.py:36
  123.9 3.1 %collective-permute-start.16 = (f32[128,128]{1,0:T(8,128)S(1)}, f32[128,128]{1,0:T(8,128)S(1)}, u32[]{:S(2)}, u32[]{:S(2)}) collective-permute-start(f32[128,128]{1,0:T(8,128)S(1)} %pad_maximum_fusion.17), channel_id=1, source_target_pairs={{0,8},{1,9},{2,10},{3,11},{4,12},{5,13},{6,14},{7,15},{8,0},{9,1},... | collective-permute-start | bytes 196616 | tf_op jit(solution)/shard_map/ppermute | solution.py:36
  127.1 5.8 %collective-permute-done.16 = f32[128,128]{1,0:T(8,128)S(1)} collective-permute-done((f32[128,128]{1,0:T(8,128)S(1)}, f32[128,128]{1,0:T(8,128)S(1)}, u32[]{:S(2)}, u32[]{:S(2)}) %collective-permute-start.16) | collective-permute-done | bytes 65568 | tf_op jit(solution)/shard_map/ppermute | solution.py:36
  132.9 1.9 collective-permute-start.17
  134.8 4.7 %collective-permute-done.17 = f32[256,128]{1,0:T(8,128)S(1)} collective-permute-done((f32[256,128]{1,0:T(8,128)S(1)}, f32[256,128]{1,0:T(8,128)S(1)}, u32[]{:S(2)}, u32[]{:S(2)}) %collective-permute-start.17) | collective-permute-done | bytes 131104 | tf_op jit(solution)/shard_map/ppermute | solution.py:36
  139.5 1.9 collective-permute-start.18
  141.5 6.3 %collective-permute-done.18 = f32[512,128]{1,0:T(8,128)S(1)} collective-permute-done((f32[512,128]{1,0:T(8,128)S(1)}, f32[512,128]{1,0:T(8,128)S(1)}, u32[]{:S(2)}, u32[]{:S(2)}) %collective-permute-start.18) | collective-permute-done | bytes 262176 | tf_op jit(solution)/shard_map/ppermute | solution.py:36
  147.8 20.3 %collective-permute-start.19 = (f32[1024,128]{1,0:T(8,128)S(1)}, f32[1024,128]{1,0:T(8,128)S(1)}, u32[]{:S(2)}, u32[]{:S(2)}) collective-permute-start(f32[1024,128]{1,0:T(8,128)S(1)} %pad_maximum_fusion.1), channel_id=1, source_target_pairs={{0,1},{1,0},{2,3},{3,2},{4,5},{5,4},{6,7},{7,6},{8,9},{9,8},{10,11... | collective-permute-start | bytes 1572872 | tf_op jit(solution)/shard_map/ppermute | solution.py:36
  170.4 11.7 %custom-call.12 = f32[128,128]{1,0:T(8,128)S(1)} custom-call(f32[128,128]{1,0:T(8,128)S(1)} %slice.90), custom_call_target="Cholesky" | custom-call | tf_op jit(solution)/shard_map/cholesky/custom-call.1 | solution.py:54
  183.5 9.8 %custom-call.13 = f32[1,128,128]{1,2,0:T(8,128)S(1)} custom-call(f32[1,128,128]{2,1,0:T(8,128)S(1)} %get-tuple-element.14), custom_call_target="InvertDiagBlocksLowerTriangular" | custom-call | tf_op jit(solution)/shard_map/triangular_solve/custom-call.0 | solution.py:55
  194.9 11.7 %custom-call.14 = f32[128,128]{1,0:T(8,128)S(1)} custom-call(f32[128,128]{1,0:T(8,128)S(1)} %slice.94), custom_call_target="Cholesky" | custom-call | tf_op jit(solution)/shard_map/cholesky/custom-call.1 | solution.py:54
  208.0 9.9 %custom-call.15 = f32[1,128,128]{1,2,0:T(8,128)S(1)} custom-call(f32[1,128,128]{2,1,0:T(8,128)S(1)} %get-tuple-element.12), custom_call_target="InvertDiagBlocksLowerTriangular" | custom-call | tf_op jit(solution)/shard_map/triangular_solve/custom-call.0 | solution.py:55
  220.5 11.7 %custom-call.16 = f32[128,128]{1,0:T(8,128)S(1)} custom-call(f32[128,128]{1,0:T(8,128)S(1)} %slice.98), custom_call_target="Cholesky" | custom-call | tf_op jit(solution)/shard_map/cholesky/custom-call.1 | solution.py:54
  233.7 9.8 %custom-call.17 = f32[1,128,128]{1,2,0:T(8,128)S(1)} custom-call(f32[1,128,128]{2,1,0:T(8,128)S(1)} %get-tuple-element.10), custom_call_target="InvertDiagBlocksLowerTriangular" | custom-call | tf_op jit(solution)/shard_map/triangular_solve/custom-call.0 | solution.py:55
  245.5 12.0 %custom-call.18 = f32[128,128]{1,0:T(8,128)S(1)} custom-call(f32[128,128]{1,0:T(8,128)S(1)} %convolution_subtract_fusion.5), custom_call_target="Cholesky" | custom-call | tf_op jit(solution)/shard_map/cholesky/custom-call.1 | solution.py:54
  258.8 9.8 %custom-call.19 = f32[1,128,128]{1,2,0:T(8,128)S(1)} custom-call(f32[1,128,128]{2,1,0:T(8,128)S(1)} %get-tuple-element.8), custom_call_target="InvertDiagBlocksLowerTriangular" | custom-call | tf_op jit(solution)/shard_map/triangular_solve/custom-call.0 | solution.py:55
  (98 shorter events, 18.9 us)
Async XLA Ops:
  3.0 17.5 %collective-permute-start = (f32[1024,128]{1,0:T(8,128)S(1)}, f32[1024,128]{1,0:T(8,128)S(1)}, u32[]{:S(2)}, u32[]{:S(2)}) collective-permute-start(f32[1024,128]{1,0:T(8,128)S(1)} %constant_dynamic-slice_fusion.12), channel_id=1, source_target_pairs={{0,1},{1,0},{2,3},{3,2},{4,5},{5,4},{6,7},{7,6},{8,9},{9,8},{10,11... | collective-permute-start | bytes 1572872 | tf_op jit(solution)/shard_map/ppermute | solution.py:32
  20.7 9.4 %collective-permute-start.1 = (f32[512,128]{1,0:T(8,128)S(1)}, f32[512,128]{1,0:T(8,128)S(1)}, u32[]{:S(2)}, u32[]{:S(2)}) collective-permute-start(f32[512,128]{1,0:T(8,128)S(1)} %constant_dynamic-slice_fusion.11), channel_id=1, source_target_pairs={{0,2},{1,3},{2,0},{3,1},{4,6},{5,7},{6,4},{7,5},{8,10},{9,11},{10,... | collective-permute-start | bytes 786440 | tf_op jit(solution)/shard_map/ppermute | solution.py:32
  30.1 11.0 %collective-permute-start.2 = (f32[256,128]{1,0:T(8,128)S(1)}, f32[256,128]{1,0:T(8,128)S(1)}, u32[]{:S(2)}, u32[]{:S(2)}) collective-permute-start(f32[256,128]{1,0:T(8,128)S(1)} %constant_dynamic-slice_fusion.10), channel_id=1, source_target_pairs={{0,4},{1,5},{2,6},{3,7},{4,0},{5,1},{6,2},{7,3},{8,12},{9,13},{10,... | collective-permute-start | bytes 393224 | tf_op jit(solution)/shard_map/ppermute | solution.py:32
  41.1 10.0 %collective-permute-start.3 = (f32[128,128]{1,0:T(8,128)S(1)}, f32[128,128]{1,0:T(8,128)S(1)}, u32[]{:S(2)}, u32[]{:S(2)}) collective-permute-start(f32[128,128]{1,0:T(8,128)S(1)} %constant_dynamic-slice_fusion.9), channel_id=1, source_target_pairs={{0,8},{1,9},{2,10},{3,11},{4,12},{5,13},{6,14},{7,15},{8,0},{9,1},... | collective-permute-start | bytes 196616 | tf_op jit(solution)/shard_map/ppermute | solution.py:32
  51.2 4.7 %collective-permute-start.4 = (f32[64,128]{1,0:T(8,128)S(1)}, f32[64,128]{1,0:T(8,128)S(1)}, u32[]{:S(2)}, u32[]{:S(2)}) collective-permute-start(f32[64,128]{1,0:T(8,128)S(1)} %constant_dynamic-slice_fusion.8), channel_id=1, source_target_pairs={{0,16},{1,17},{2,18},{3,19},{4,20},{5,21},{6,22},{7,23},{8,24},{9,... | collective-permute-start | bytes 98312 | tf_op jit(solution)/shard_map/ppermute | solution.py:32
  55.9 5.4 %collective-permute-start.5 = (f32[32,128]{1,0:T(8,128)S(1)}, f32[32,128]{1,0:T(8,128)S(1)}, u32[]{:S(2)}, u32[]{:S(2)}) collective-permute-start(f32[32,128]{1,0:T(8,128)S(1)} %constant_dynamic-slice_fusion.7), channel_id=1, source_target_pairs={{0,32},{1,33},{2,34},{3,35},{4,36},{5,37},{6,38},{7,39},{8,40},{9,... | collective-permute-start | bytes 49160 | tf_op jit(solution)/shard_map/ppermute | solution.py:32
  61.3 8.3 %collective-permute-start.6 = (f32[16,128]{1,0:T(8,128)S(1)}, f32[16,128]{1,0:T(8,128)S(1)}, u32[]{:S(2)}, u32[]{:S(2)}) collective-permute-start(f32[16,128]{1,0:T(8,128)S(1)} %constant_dynamic-slice_fusion.6), channel_id=1, source_target_pairs={{0,64},{1,65},{2,66},{3,67},{4,68},{5,69},{6,70},{7,71},{8,72},{9,... | collective-permute-start | bytes 24584 | tf_op jit(solution)/shard_map/ppermute | solution.py:32
  69.6 4.3 %collective-permute-start.7 = (f32[8,128]{1,0:T(8,128)S(1)}, f32[8,128]{1,0:T(8,128)S(1)}, u32[]{:S(2)}, u32[]{:S(2)}) collective-permute-start(f32[8,128]{1,0:T(8,128)S(1)} %constant_dynamic-slice_fusion.4), channel_id=1, source_target_pairs={{0,128},{1,129},{2,130},{3,131},{4,132},{5,133},{6,134},{7,135},{8... | collective-permute-start | bytes 12296 | tf_op jit(solution)/shard_map/ppermute | solution.py:32
  73.9 5.2 %collective-permute-start.8 = (f32[4,128]{1,0:T(4,128)S(1)}, f32[4,128]{1,0:T(4,128)S(1)}, u32[]{:S(2)}, u32[]{:S(2)}) collective-permute-start(f32[4,128]{1,0:T(4,128)S(1)} %constant_dynamic-slice_fusion.2), channel_id=1, source_target_pairs={{0,256},{1,257},{2,258},{3,259},{4,260},{5,261},{6,262},{7,263},{8... | collective-permute-start | bytes 6152 | tf_op jit(solution)/shard_map/ppermute | solution.py:32
  79.2 8.2 %collective-permute-start.9 = (f32[2,128]{1,0:T(2,128)S(1)}, f32[2,128]{1,0:T(2,128)S(1)}, u32[]{:S(2)}, u32[]{:S(2)}) collective-permute-start(f32[2,128]{1,0:T(2,128)S(1)} %constant_dynamic-slice_fusion), channel_id=1, source_target_pairs={{0,512},{1,513},{2,514},{3,515},{4,516},{5,517},{6,518},{7,519},{8... | collective-permute-start | bytes 3080 | tf_op jit(solution)/shard_map/ppermute | solution.py:32
  87.4 8.2 %collective-permute-start.10 = (f32[2,128]{1,0:T(2,128)S(1)}, f32[2,128]{1,0:T(2,128)S(1)}, u32[]{:S(2)}, u32[]{:S(2)}) collective-permute-start(f32[2,128]{1,0:T(2,128)S(1)} %fusion.58), channel_id=1, source_target_pairs={{0,512},{1,513},{2,514},{3,515},{4,516},{5,517},{6,518},{7,519},{8... | collective-permute-start | bytes 3080 | tf_op jit(solution)/shard_map/ppermute | solution.py:36
  95.6 5.2 %collective-permute-start.11 = (f32[4,128]{1,0:T(4,128)S(1)}, f32[4,128]{1,0:T(4,128)S(1)}, u32[]{:S(2)}, u32[]{:S(2)}) collective-permute-start(f32[4,128]{1,0:T(4,128)S(1)} %pad_maximum_fusion.22), channel_id=1, source_target_pairs={{0,256},{1,257},{2,258},{3,259},{4,260},{5,261},{6,262},{7,263},{8... | collective-permute-start | bytes 6152 | tf_op jit(solution)/shard_map/ppermute | solution.py:36
  100.9 4.4 %collective-permute-start.12 = (f32[8,128]{1,0:T(8,128)S(1)}, f32[8,128]{1,0:T(8,128)S(1)}, u32[]{:S(2)}, u32[]{:S(2)}) collective-permute-start(f32[8,128]{1,0:T(8,128)S(1)} %pad_maximum_fusion.21), channel_id=1, source_target_pairs={{0,128},{1,129},{2,130},{3,131},{4,132},{5,133},{6,134},{7,135},{8... | collective-permute-start | bytes 12296 | tf_op jit(solution)/shard_map/ppermute | solution.py:36
  105.3 8.3 %collective-permute-start.13 = (f32[16,128]{1,0:T(8,128)S(1)}, f32[16,128]{1,0:T(8,128)S(1)}, u32[]{:S(2)}, u32[]{:S(2)}) collective-permute-start(f32[16,128]{1,0:T(8,128)S(1)} %pad_maximum_fusion.20), channel_id=1, source_target_pairs={{0,64},{1,65},{2,66},{3,67},{4,68},{5,69},{6,70},{7,71},{8,72},{9,... | collective-permute-start | bytes 24584 | tf_op jit(solution)/shard_map/ppermute | solution.py:36
  113.6 5.4 %collective-permute-start.14 = (f32[32,128]{1,0:T(8,128)S(1)}, f32[32,128]{1,0:T(8,128)S(1)}, u32[]{:S(2)}, u32[]{:S(2)}) collective-permute-start(f32[32,128]{1,0:T(8,128)S(1)} %pad_maximum_fusion.19), channel_id=1, source_target_pairs={{0,32},{1,33},{2,34},{3,35},{4,36},{5,37},{6,38},{7,39},{8,40},{9,... | collective-permute-start | bytes 49160 | tf_op jit(solution)/shard_map/ppermute | solution.py:36
  119.0 5.0 %collective-permute-start.15 = (f32[64,128]{1,0:T(8,128)S(1)}, f32[64,128]{1,0:T(8,128)S(1)}, u32[]{:S(2)}, u32[]{:S(2)}) collective-permute-start(f32[64,128]{1,0:T(8,128)S(1)} %pad_maximum_fusion.18), channel_id=1, source_target_pairs={{0,16},{1,17},{2,18},{3,19},{4,20},{5,21},{6,22},{7,23},{8,24},{9,... | collective-permute-start | bytes 98312 | tf_op jit(solution)/shard_map/ppermute | solution.py:36
  123.9 8.9 %collective-permute-start.16 = (f32[128,128]{1,0:T(8,128)S(1)}, f32[128,128]{1,0:T(8,128)S(1)}, u32[]{:S(2)}, u32[]{:S(2)}) collective-permute-start(f32[128,128]{1,0:T(8,128)S(1)} %pad_maximum_fusion.17), channel_id=1, source_target_pairs={{0,8},{1,9},{2,10},{3,11},{4,12},{5,13},{6,14},{7,15},{8,0},{9,1},... | collective-permute-start | bytes 196616 | tf_op jit(solution)/shard_map/ppermute | solution.py:36
  132.9 6.6 %collective-permute-start.17 = (f32[256,128]{1,0:T(8,128)S(1)}, f32[256,128]{1,0:T(8,128)S(1)}, u32[]{:S(2)}, u32[]{:S(2)}) collective-permute-start(f32[256,128]{1,0:T(8,128)S(1)} %pad_maximum_fusion.16), channel_id=1, source_target_pairs={{0,4},{1,5},{2,6},{3,7},{4,0},{5,1},{6,2},{7,3},{8,12},{9,13},{10,... | collective-permute-start | bytes 393224 | tf_op jit(solution)/shard_map/ppermute | solution.py:36
  139.5 8.2 %collective-permute-start.18 = (f32[512,128]{1,0:T(8,128)S(1)}, f32[512,128]{1,0:T(8,128)S(1)}, u32[]{:S(2)}, u32[]{:S(2)}) collective-permute-start(f32[512,128]{1,0:T(8,128)S(1)} %pad_maximum_fusion.2), channel_id=1, source_target_pairs={{0,2},{1,3},{2,0},{3,1},{4,6},{5,7},{6,4},{7,5},{8,10},{9,11},{10,... | collective-permute-start | bytes 786440 | tf_op jit(solution)/shard_map/ppermute | solution.py:36
  147.8 21.7 %collective-permute-start.19 = (f32[1024,128]{1,0:T(8,128)S(1)}, f32[1024,128]{1,0:T(8,128)S(1)}, u32[]{:S(2)}, u32[]{:S(2)}) collective-permute-start(f32[1024,128]{1,0:T(8,128)S(1)} %pad_maximum_fusion.1), channel_id=1, source_target_pairs={{0,1},{1,0},{2,3},{3,2},{4,5},{5,4},{6,7},{7,6},{8,9},{9,8},{10,11... | collective-permute-start | bytes 1572872 | tf_op jit(solution)/shard_map/ppermute | solution.py:36
  170.4 23.2 %copy-start = (f32[256,512]{1,0:T(8,128)S(1)}, f32[256,512]{1,0:T(8,128)}, u32[]{:S(2)}) copy-start(f32[256,512]{1,0:T(8,128)} %param.4) | copy-start | bytes 1572868
  194.3 24.3 %copy-start.1 = (f32[384,128]{0,1:T(8,128)}, f32[384,128]{0,1:T(8,128)S(1)}, u32[]{:S(2)}) copy-start(f32[384,128]{0,1:T(8,128)S(1)} %fusion.21) | copy-start | bytes 589828
  218.5 0.8 copy-start.2
  219.0 0.9 slice-start.1
  244.1 0.8 slice-start
  244.1 0.9 slice-start.2

commit v3 on v2

--- a/solution.py
+++ b/solution.py
@@ -16,10 +16,11 @@
 
 
 def summed(gram):
-    n_dev = lax.axis_size("rows") * lax.axis_size("chip")
-    steps = int(math.log2(n_dev))
-    assert 1 << steps == n_dev
-    me = lax.axis_index(AXES)
+    n_chip = lax.axis_size("chip")
+    n_rows = lax.axis_size("rows")
+    steps = int(math.log2(n_chip))
+    assert 1 << steps == n_chip
+    me = lax.axis_index("chip")
     shape = gram.shape
     x = gram.reshape(-1, 128)
     masks = [1 << k for k in range(steps)]
@@ -28,12 +29,16 @@
         bit = (me // m) % 2
         keep = lax.dynamic_slice_in_dim(x, bit * half, half, 0)
         send = lax.dynamic_slice_in_dim(x, (1 - bit) * half, half, 0)
-        perm = [(i, i ^ m) for i in range(n_dev)]
-        x = keep + lax.ppermute(send, AXES, perm)
+        perm = [(i, i ^ m) for i in range(n_chip)]
+        x = keep + lax.ppermute(send, "chip", perm)
+    part = x.shape[0] // n_rows
+    got = lax.all_to_all(x, "rows", 0, 0, tiled=True)
+    x = jnp.sum(got.reshape(n_rows, part, 128), axis=0)
+    x = lax.all_to_all(jnp.tile(x, (n_rows, 1)), "rows", 0, 0, tiled=True)
     for m in reversed(masks):
         bit = (me // m) % 2
-        perm = [(i, i ^ m) for i in range(n_dev)]
-        other = lax.ppermute(x, AXES, perm)
+        perm = [(i, i ^ m) for i in range(n_chip)]
+        other = lax.ppermute(x, "chip", perm)
         lo = jnp.where(bit == 0, x, other)
         hi = jnp.where(bit == 0, other, x)
         x = jnp.concatenate([lo, hi], axis=0)

time: 274 us -> 225 us (0.82)
  waiting for transfers between devices: 87.5 us -> 37.4 us
  blocking collectives: 0 us -> 33.9 us
  starting transfers between devices: 77.8 us -> 45.8 us
    ppermute x20 -> x8, waiting for transfers between devices: 87.5 us -> 37.4 us  [the longest x4 24.7 us: summed(): x = keep + lax.ppermute(send, 'chip', perm)]
    all_to_all x0 -> x2, blocking collectives: none -> 33.9 us  [the longest x1 19 us: summed(): got = lax.all_to_all(x, 'rows', 0, 0, tiled=True)]
    ppermute x20 -> x8, starting transfers between devices: 77.8 us -> 45.8 us  [the longest x4 23.1 us: summed(): x = keep + lax.ppermute(send, 'chip', perm)]
  transfers between devices with their start and end apart: 20 -> 8, of which waited for: 20 -> 8; matrix products, arithmetic and copies ran while one was open for 0% -> 0% of each run, Pallas kernels for 0% -> 0%
where the time goes in v3:
time: 225 us
  other arithmetic  92.7 us (41%)
  starting transfers between devices  45.8 us (20%)
  waiting for transfers between devices  37.4 us (17%)
  blocking collectives  33.9 us (15%)
  matrix products  8.78 us (4%)
  local copies, waits for them, and re-layouts  4.71 us (2%)
    another operation x12, other arithmetic, factor(): diag = lax.linalg.cholesky(rest[:BLOCK], symmetrize_input=False)  49.9 us
    another operation x8, other arithmetic, factor(): lax.linalg.triangular_solve(diag, jnp.eye(BLOCK, dtype=diag.dtype), left_...  42 us
    ppermute x4, waiting for transfers between devices, summed(): x = keep + lax.ppermute(send, 'chip', perm)  24.7 us
    ppermute x4, starting transfers between devices, summed(): x = keep + lax.ppermute(send, 'chip', perm)  23.1 us
    ppermute x4, starting transfers between devices, summed(): other = lax.ppermute(x, 'chip', perm)  22.7 us
    all_to_all x1, blocking collectives, summed(): got = lax.all_to_all(x, 'rows', 0, 0, tiled=True)  19 us
    all_to_all x1, blocking collectives, summed(): x = lax.all_to_all(jnp.tile(x, (n_rows, 1)), 'rows', 0, 0, tiled=True)  14.9 us
    ppermute x4, waiting for transfers between devices, summed(): other = lax.ppermute(x, 'chip', perm)  12.8 us
  transfers between devices with their start and end apart: 8, of which 8 were waited for; matrix products, arithmetic and copies ran while one was open for 0% of the time, Pallas kernels for 0%

profile of v3, /device:TPU:1, one launch (start us, length us, event | category | flops | bytes accessed | tf_op | source)
XLA Modules:
  0.0 224.7 jit_solution(16801152986030796425)
XLA Ops:
  0.6 2.2 fusion.61
  3.0 16.0 %collective-permute-start = (f32[1024,128]{1,0:T(8,128)S(1)}, f32[1024,128]{1,0:T(8,128)S(1)}, u32[]{:S(2)}, u32[]{:S(2)}) collective-permute-start(f32[1024,128]{1,0:T(8,128)S(1)} %constant_dynamic-slice_fusion.3), channel_id=1, source_target_pairs={{0,1},{1,0},{2,3},{3,2},{4,5},{5,4},{6,7},{7,6},{8,9},{9,8},{10,11... | collective-permute-start | bytes 1572872 | tf_op jit(solution)/shard_map/ppermute | solution.py:33
  19.1 1.5 collective-permute-done
  20.6 1.9 collective-permute-start.1
  22.6 7.4 %collective-permute-done.1 = f32[512,128]{1,0:T(8,128)S(1)} collective-permute-done((f32[512,128]{1,0:T(8,128)S(1)}, f32[512,128]{1,0:T(8,128)S(1)}, u32[]{:S(2)}, u32[]{:S(2)}) %collective-permute-start.1) | collective-permute-done | bytes 262176 | tf_op jit(solution)/shard_map/ppermute | solution.py:33
  30.1 1.9 collective-permute-start.2
  32.1 9.0 %collective-permute-done.2 = f32[256,128]{1,0:T(8,128)S(1)} collective-permute-done((f32[256,128]{1,0:T(8,128)S(1)}, f32[256,128]{1,0:T(8,128)S(1)}, u32[]{:S(2)}, u32[]{:S(2)}) %collective-permute-start.2) | collective-permute-done | bytes 131104 | tf_op jit(solution)/shard_map/ppermute | solution.py:33
  41.1 3.3 %collective-permute-start.3 = (f32[128,128]{1,0:T(8,128)S(1)}, f32[128,128]{1,0:T(8,128)S(1)}, u32[]{:S(2)}, u32[]{:S(2)}) collective-permute-start(f32[128,128]{1,0:T(8,128)S(1)} %constant_dynamic-slice_fusion), channel_id=1, source_target_pairs={{0,8},{1,9},{2,10},{3,11},{4,12},{5,13},{6,14},{7,15},{8,0},{9,1},... | collective-permute-start | bytes 196616 | tf_op jit(solution)/shard_map/ppermute | solution.py:33
  44.4 6.7 %collective-permute-done.3 = f32[128,128]{1,0:T(8,128)S(1)} collective-permute-done((f32[128,128]{1,0:T(8,128)S(1)}, f32[128,128]{1,0:T(8,128)S(1)}, u32[]{:S(2)}, u32[]{:S(2)}) %collective-permute-start.3) | collective-permute-done | bytes 65568 | tf_op jit(solution)/shard_map/ppermute | solution.py:33
  51.2 19.0 %all_to_all.18 = f32[64,2,128]{2,1,0:T(2,128)S(1)} all-to-all(f32[64,2,128]{2,1,0:T(2,128)S(1)} %bitcast.46), channel_id=1, replica_groups=mesh['rows'=64,'chip'=16] {'rows'}, dimensions={0} | all-to-all | bytes 131072 | tf_op jit(solution)/shard_map/all_to_all | solution.py:35
  70.3 14.9 %all_to_all.19 = f32[64,2,128]{2,1,0:T(2,128)S(1)} all-to-all(f32[64,2,128]{2,1,0:T(2,128)S(1)} %tile.2), channel_id=1, replica_groups=mesh['rows'=64,'chip'=16] {'rows'}, dimensions={0} | all-to-all | bytes 131072 | tf_op jit(solution)/shard_map/all_to_all | solution.py:37
  85.2 7.4 %collective-permute-start.4 = (f32[128,128]{1,0:T(8,128)S(1)}, f32[128,128]{1,0:T(8,128)S(1)}, u32[]{:S(2)}, u32[]{:S(2)}) collective-permute-start(f32[128,128]{1,0:T(8,128)S(1)} %bitcast.47), channel_id=1, source_target_pairs={{0,8},{1,9},{2,10},{3,11},{4,12},{5,13},{6,14},{7,15},{8,0},{9,1},... | collective-permute-start | bytes 196616 | tf_op jit(solution)/shard_map/ppermute | solution.py:41
  92.6 1.6 collective-permute-done.4
  94.3 1.9 collective-permute-start.5
  96.2 4.9 %collective-permute-done.5 = f32[256,128]{1,0:T(8,128)S(1)} collective-permute-done((f32[256,128]{1,0:T(8,128)S(1)}, f32[256,128]{1,0:T(8,128)S(1)}, u32[]{:S(2)}, u32[]{:S(2)}) %collective-permute-start.5) | collective-permute-done | bytes 131104 | tf_op jit(solution)/shard_map/ppermute | solution.py:41
  101.1 4.0 %collective-permute-start.6 = (f32[512,128]{1,0:T(8,128)S(1)}, f32[512,128]{1,0:T(8,128)S(1)}, u32[]{:S(2)}, u32[]{:S(2)}) collective-permute-start(f32[512,128]{1,0:T(8,128)S(1)} %pad_maximum_fusion.2), channel_id=1, source_target_pairs={{0,2},{1,3},{2,0},{3,1},{4,6},{5,7},{6,4},{7,5},{8,10},{9,11},{10,... | collective-permute-start | bytes 786440 | tf_op jit(solution)/shard_map/ppermute | solution.py:41
  105.1 4.9 %collective-permute-done.6 = f32[512,128]{1,0:T(8,128)S(1)} collective-permute-done((f32[512,128]{1,0:T(8,128)S(1)}, f32[512,128]{1,0:T(8,128)S(1)}, u32[]{:S(2)}, u32[]{:S(2)}) %collective-permute-start.6) | collective-permute-done | bytes 262176 | tf_op jit(solution)/shard_map/ppermute | solution.py:41
  110.1 9.4 %collective-permute-start.7 = (f32[1024,128]{1,0:T(8,128)S(1)}, f32[1024,128]{1,0:T(8,128)S(1)}, u32[]{:S(2)}, u32[]{:S(2)}) collective-permute-start(f32[1024,128]{1,0:T(8,128)S(1)} %pad_maximum_fusion.1), channel_id=1, source_target_pairs={{0,1},{1,0},{2,3},{3,2},{4,5},{5,4},{6,7},{7,6},{8,9},{9,8},{10,11... | collective-permute-start | bytes 1572872 | tf_op jit(solution)/shard_map/ppermute | solution.py:41
  119.5 1.3 collective-permute-done.7
  121.2 0.3 copy.9
  121.8 11.7 %custom-call.12 = f32[128,128]{1,0:T(8,128)S(1)} custom-call(f32[128,128]{1,0:T(8,128)S(1)} %slice.90), custom_call_target="Cholesky" | custom-call | tf_op jit(solution)/shard_map/cholesky/custom-call.1 | solution.py:59
  133.5 0.6 compare_reduce_fusion.3
  134.2 0.7 select_bitcast_fusion.3
  134.8 9.8 %custom-call.13 = f32[1,128,128]{1,2,0:T(8,128)S(1)} custom-call(f32[1,128,128]{2,1,0:T(8,128)S(1)} %get-tuple-element.14), custom_call_target="InvertDiagBlocksLowerTriangular" | custom-call | tf_op jit(solution)/shard_map/triangular_solve/custom-call.0 | solution.py:60
  145.2 0.4 fusion.21
  145.8 0.5 convolution_subtract_fusion
  146.3 11.7 %custom-call.14 = f32[128,128]{1,0:T(8,128)S(1)} custom-call(f32[128,128]{1,0:T(8,128)S(1)} %slice.94), custom_call_target="Cholesky" | custom-call | tf_op jit(solution)/shard_map/cholesky/custom-call.1 | solution.py:59
  158.0 0.6 compare_reduce_fusion.2
  158.7 0.7 select_bitcast_fusion.2
  159.3 9.9 %custom-call.15 = f32[1,128,128]{1,2,0:T(8,128)S(1)} custom-call(f32[1,128,128]{2,1,0:T(8,128)S(1)} %get-tuple-element.12), custom_call_target="InvertDiagBlocksLowerTriangular" | custom-call | tf_op jit(solution)/shard_map/triangular_solve/custom-call.0 | solution.py:60
  170.0 0.4 convolution_subtract_fusion.4
  170.7 0.6 slice-done.1
  171.3 0.6 convolution_subtract_fusion.2
  171.9 11.7 %custom-call.16 = f32[128,128]{1,0:T(8,128)S(1)} custom-call(f32[128,128]{1,0:T(8,128)S(1)} %slice.98), custom_call_target="Cholesky" | custom-call | tf_op jit(solution)/shard_map/cholesky/custom-call.1 | solution.py:59
  183.6 0.7 compare_reduce_fusion.1
  184.3 0.7 select_bitcast_fusion.1
  185.1 9.8 %custom-call.17 = f32[1,128,128]{1,2,0:T(8,128)S(1)} custom-call(f32[1,128,128]{2,1,0:T(8,128)S(1)} %get-tuple-element.10), custom_call_target="InvertDiagBlocksLowerTriangular" | custom-call | tf_op jit(solution)/shard_map/triangular_solve/custom-call.0 | solution.py:60
  194.9 0.3 fusion.30
  195.5 0.7 slice-done
  196.3 0.5 convolution_subtract_fusion.5
  196.8 12.0 %custom-call.18 = f32[128,128]{1,0:T(8,128)S(1)} custom-call(f32[128,128]{1,0:T(8,128)S(1)} %convolution_subtract_fusion.5), custom_call_target="Cholesky" | custom-call | tf_op jit(solution)/shard_map/cholesky/custom-call.1 | solution.py:59
  208.8 0.6 compare_reduce_fusion
  209.4 0.7 select_bitcast_fusion
  210.1 9.8 %custom-call.19 = f32[1,128,128]{1,2,0:T(8,128)S(1)} custom-call(f32[1,128,128]{2,1,0:T(8,128)S(1)} %get-tuple-element.8), custom_call_target="InvertDiagBlocksLowerTriangular" | custom-call | tf_op jit(solution)/shard_map/triangular_solve/custom-call.0 | solution.py:60
  220.2 0.6 convolution_subtract_fusion.3
  221.1 0.8 convolution_subtract_fusion.1
  222.3 1.0 copy.13
  223.4 1.3 copy.14
  (54 shorter events, 4.2 us)
Async XLA Ops:
  3.0 17.5 %collective-permute-start = (f32[1024,128]{1,0:T(8,128)S(1)}, f32[1024,128]{1,0:T(8,128)S(1)}, u32[]{:S(2)}, u32[]{:S(2)}) collective-permute-start(f32[1024,128]{1,0:T(8,128)S(1)} %constant_dynamic-slice_fusion.3), channel_id=1, source_target_pairs={{0,1},{1,0},{2,3},{3,2},{4,5},{5,4},{6,7},{7,6},{8,9},{9,8},{10,11... | collective-permute-start | bytes 1572872 | tf_op jit(solution)/shard_map/ppermute | solution.py:33
  20.6 9.4 %collective-permute-start.1 = (f32[512,128]{1,0:T(8,128)S(1)}, f32[512,128]{1,0:T(8,128)S(1)}, u32[]{:S(2)}, u32[]{:S(2)}) collective-permute-start(f32[512,128]{1,0:T(8,128)S(1)} %constant_dynamic-slice_fusion.2), channel_id=1, source_target_pairs={{0,2},{1,3},{2,0},{3,1},{4,6},{5,7},{6,4},{7,5},{8,10},{9,11},{10,... | collective-permute-start | bytes 786440 | tf_op jit(solution)/shard_map/ppermute | solution.py:33
  30.1 11.0 %collective-permute-start.2 = (f32[256,128]{1,0:T(8,128)S(1)}, f32[256,128]{1,0:T(8,128)S(1)}, u32[]{:S(2)}, u32[]{:S(2)}) collective-permute-start(f32[256,128]{1,0:T(8,128)S(1)} %constant_dynamic-slice_fusion.1), channel_id=1, source_target_pairs={{0,4},{1,5},{2,6},{3,7},{4,0},{5,1},{6,2},{7,3},{8,12},{9,13},{10,... | collective-permute-start | bytes 393224 | tf_op jit(solution)/shard_map/ppermute | solution.py:33
  41.1 10.0 %collective-permute-start.3 = (f32[128,128]{1,0:T(8,128)S(1)}, f32[128,128]{1,0:T(8,128)S(1)}, u32[]{:S(2)}, u32[]{:S(2)}) collective-permute-start(f32[128,128]{1,0:T(8,128)S(1)} %constant_dynamic-slice_fusion), channel_id=1, source_target_pairs={{0,8},{1,9},{2,10},{3,11},{4,12},{5,13},{6,14},{7,15},{8,0},{9,1},... | collective-permute-start | bytes 196616 | tf_op jit(solution)/shard_map/ppermute | solution.py:33
  85.2 9.0 %collective-permute-start.4 = (f32[128,128]{1,0:T(8,128)S(1)}, f32[128,128]{1,0:T(8,128)S(1)}, u32[]{:S(2)}, u32[]{:S(2)}) collective-permute-start(f32[128,128]{1,0:T(8,128)S(1)} %bitcast.47), channel_id=1, source_target_pairs={{0,8},{1,9},{2,10},{3,11},{4,12},{5,13},{6,14},{7,15},{8,0},{9,1},... | collective-permute-start | bytes 196616 | tf_op jit(solution)/shard_map/ppermute | solution.py:41
  94.3 6.8 %collective-permute-start.5 = (f32[256,128]{1,0:T(8,128)S(1)}, f32[256,128]{1,0:T(8,128)S(1)}, u32[]{:S(2)}, u32[]{:S(2)}) collective-permute-start(f32[256,128]{1,0:T(8,128)S(1)} %pad_maximum_fusion.16), channel_id=1, source_target_pairs={{0,4},{1,5},{2,6},{3,7},{4,0},{5,1},{6,2},{7,3},{8,12},{9,13},{10,... | collective-permute-start | bytes 393224 | tf_op jit(solution)/shard_map/ppermute | solution.py:41
  101.1 8.9 %collective-permute-start.6 = (f32[512,128]{1,0:T(8,128)S(1)}, f32[512,128]{1,0:T(8,128)S(1)}, u32[]{:S(2)}, u32[]{:S(2)}) collective-permute-start(f32[512,128]{1,0:T(8,128)S(1)} %pad_maximum_fusion.2), channel_id=1, source_target_pairs={{0,2},{1,3},{2,0},{3,1},{4,6},{5,7},{6,4},{7,5},{8,10},{9,11},{10,... | collective-permute-start | bytes 786440 | tf_op jit(solution)/shard_map/ppermute | solution.py:41
  110.1 10.8 %collective-permute-start.7 = (f32[1024,128]{1,0:T(8,128)S(1)}, f32[1024,128]{1,0:T(8,128)S(1)}, u32[]{:S(2)}, u32[]{:S(2)}) collective-permute-start(f32[1024,128]{1,0:T(8,128)S(1)} %pad_maximum_fusion.1), channel_id=1, source_target_pairs={{0,1},{1,0},{2,3},{3,2},{4,5},{5,4},{6,7},{7,6},{8,9},{9,8},{10,11... | collective-permute-start | bytes 1572872 | tf_op jit(solution)/shard_map/ppermute | solution.py:41
  121.7 23.2 %copy-start = (f32[256,512]{1,0:T(8,128)S(1)}, f32[256,512]{1,0:T(8,128)}, u32[]{:S(2)}) copy-start(f32[256,512]{1,0:T(8,128)} %param.4) | copy-start | bytes 1572868
  145.6 24.3 %copy-start.1 = (f32[384,128]{0,1:T(8,128)}, f32[384,128]{0,1:T(8,128)S(1)}, u32[]{:S(2)}) copy-start(f32[384,128]{0,1:T(8,128)S(1)} %fusion.21) | copy-start | bytes 589828
  169.8 0.8 copy-start.2
  170.4 0.9 slice-start.1
  195.4 0.8 slice-start
  195.4 0.9 slice-start.2

commit v4 on v2

--- a/solution.py
+++ b/solution.py
@@ -16,27 +16,15 @@
 
 
 def summed(gram):
-    n_dev = lax.axis_size("rows") * lax.axis_size("chip")
-    steps = int(math.log2(n_dev))
-    assert 1 << steps == n_dev
-    me = lax.axis_index(AXES)
+    n_rows = lax.axis_size("rows")
+    n_chip = lax.axis_size("chip")
     shape = gram.shape
     x = gram.reshape(-1, 128)
-    masks = [1 << k for k in range(steps)]
-    for m in masks:
-        half = x.shape[0] // 2
-        bit = (me // m) % 2
-        keep = lax.dynamic_slice_in_dim(x, bit * half, half, 0)
-        send = lax.dynamic_slice_in_dim(x, (1 - bit) * half, half, 0)
-        perm = [(i, i ^ m) for i in range(n_dev)]
-        x = keep + lax.ppermute(send, AXES, perm)
-    for m in reversed(masks):
-        bit = (me // m) % 2
-        perm = [(i, i ^ m) for i in range(n_dev)]
-        other = lax.ppermute(x, AXES, perm)
-        lo = jnp.where(bit == 0, x, other)
-        hi = jnp.where(bit == 0, other, x)
-        x = jnp.concatenate([lo, hi], axis=0)
+    for axis, n in (("rows", n_rows), ("chip", n_chip)):
+        got = lax.all_to_all(x, axis, 0, 0, tiled=True)
+        x = jnp.sum(got.reshape(n, x.shape[0] // n, 128), axis=0)
+    for axis, n in (("chip", n_chip), ("rows", n_rows)):
+        x = lax.all_to_all(jnp.tile(x, (n, 1)), axis, 0, 0, tiled=True)
     return x.reshape(shape)
 
 

time: 274 us -> 221 us (0.81)
  blocking collectives: 0 us -> 111 us
  waiting for transfers between devices: 87.5 us -> 0 us
  starting transfers between devices: 77.8 us -> 0 us
    all_to_all x0 -> x4, blocking collectives: none -> 111 us  [the longest x2 68.1 us: summed(): got = lax.all_to_all(x, axis, 0, 0, tiled=True)]
    ppermute x20 -> x0, waiting for transfers between devices: 87.5 us -> none  [the longest x10 47.1 us: summed(): x = keep + lax.ppermute(send, AXES, perm)]
    ppermute x20 -> x0, starting transfers between devices: 77.8 us -> none  [the longest x10 41.3 us: summed(): other = lax.ppermute(x, AXES, perm)]
  transfers between devices with their start and end apart: 20 -> 0, of which waited for: 20 -> 0; matrix products, arithmetic and copies ran while one was open for 0% -> 0% of each run, Pallas kernels for 0% -> 0%
where the time goes in v4:
time: 221 us; the launch traced here: 218 us
  blocking collectives  111 us (50%)
  other arithmetic  92.4 us (42%)
  matrix products  8.78 us (4%)
  local copies, waits for them, and re-layouts  4.72 us (2%)
    all_to_all x2, blocking collectives, summed(): got = lax.all_to_all(x, axis, 0, 0, tiled=True)  68.1 us
    another operation x12, other arithmetic, factor(): diag = lax.linalg.cholesky(rest[:BLOCK], symmetrize_input=False)  49.9 us
    all_to_all x2, blocking collectives, summed(): x = lax.all_to_all(jnp.tile(x, (n, 1)), axis, 0, 0, tiled=True)  43.2 us
    another operation x8, other arithmetic, factor(): lax.linalg.triangular_solve(diag, jnp.eye(BLOCK, dtype=diag.dtype), left_...  42.1 us
    dot_general x14, matrix products, mm(): lax.dot_general(a, b, (dims, ((), ())), precision=lax.Precision.HIGHEST,...  7.63 us

profile of v4, /device:TPU:1, one launch (start us, length us, event | category | flops | bytes accessed | tf_op | source)
XLA Modules:
  0.0 218.2 jit_solution(6950765044694878704)
XLA Ops:
  0.6 2.2 %fusion.61 = f32[512,512]{1,0:T(8,128)S(1)} fusion(f32[256,512]{1,0:T(8,128)} %param.4), kind=kOutput, calls=%fused_computation.92 | convolution fusion | flops 805306368 | bytes 1572864 | tf_op jit(solution)/shard_map/dot_general | solution.py:13
  2.9 37.2 %all_to_all.30 = f32[64,32,128]{2,1,0:T(8,128)S(1)} all-to-all(f32[64,32,128]{2,1,0:T(8,128)S(1)} %all_to_all.20), channel_id=1, replica_groups=mesh['rows'=64,'chip'=16] {'rows'}, dimensions={0} | all-to-all | bytes 2097152 | tf_op jit(solution)/shard_map/all_to_all | solution.py:24
  40.2 0.1 reduce_sum.18
  40.3 30.9 %all_to_all.31 = f32[16,2,128]{2,1,0:T(2,128)S(1)} all-to-all(f32[16,2,128]{2,1,0:T(2,128)S(1)} %bitcast.46), channel_id=1, replica_groups=mesh['rows'=64,'chip'=16] {'chip'}, dimensions={0} | all-to-all | bytes 32768 | tf_op jit(solution)/shard_map/all_to_all | solution.py:24
  71.2 10.2 %all_to_all.32 = f32[16,2,128]{2,1,0:T(2,128)S(1)} all-to-all(f32[16,2,128]{2,1,0:T(2,128)S(1)} %tile.6), channel_id=1, replica_groups=mesh['rows'=64,'chip'=16] {'chip'}, dimensions={0} | all-to-all | bytes 32768 | tf_op jit(solution)/shard_map/all_to_all | solution.py:27
  81.3 0.1 tile.8
  81.4 33.0 %all_to_all.33 = f32[64,32,128]{2,1,0:T(8,128)S(1)} all-to-all(f32[64,32,128]{2,1,0:T(8,128)S(1)} %tile.8), channel_id=1, replica_groups=mesh['rows'=64,'chip'=16] {'rows'}, dimensions={0} | all-to-all | bytes 2097152 | tf_op jit(solution)/shard_map/all_to_all | solution.py:27
  114.5 0.2 reshape.43
  114.6 0.3 copy.22
  115.0 0.2 fusion.2
  115.2 11.7 %custom-call.12 = f32[128,128]{1,0:T(8,128)S(1)} custom-call(f32[128,128]{1,0:T(8,128)S(1)} %slice.90), custom_call_target="Cholesky" | custom-call | tf_op jit(solution)/shard_map/cholesky/custom-call.1 | solution.py:42
  127.0 0.6 compare_reduce_fusion.3
  127.6 0.7 select_bitcast_fusion.3
  128.3 9.8 %custom-call.13 = f32[1,128,128]{1,2,0:T(8,128)S(1)} custom-call(f32[1,128,128]{2,1,0:T(8,128)S(1)} %get-tuple-element.18), custom_call_target="InvertDiagBlocksLowerTriangular" | custom-call | tf_op jit(solution)/shard_map/triangular_solve/custom-call.0 | solution.py:43
  138.1 0.3 fusion.34
  138.4 0.3 fusion.45
  138.7 0.4 fusion.21
  139.1 0.1 copy.23
  139.2 0.5 convolution_subtract_fusion
  139.7 11.7 %custom-call.14 = f32[128,128]{1,0:T(8,128)S(1)} custom-call(f32[128,128]{1,0:T(8,128)S(1)} %slice.94), custom_call_target="Cholesky" | custom-call | tf_op jit(solution)/shard_map/cholesky/custom-call.1 | solution.py:42
  151.5 0.6 compare_reduce_fusion.2
  152.1 0.7 select_bitcast_fusion.2
  152.8 10.0 %custom-call.15 = f32[1,128,128]{1,2,0:T(8,128)S(1)} custom-call(f32[1,128,128]{2,1,0:T(8,128)S(1)} %get-tuple-element.16), custom_call_target="InvertDiagBlocksLowerTriangular" | custom-call | tf_op jit(solution)/shard_map/triangular_solve/custom-call.0 | solution.py:43
  162.8 0.3 fusion.32
  163.1 0.3 fusion.43
  163.5 0.4 convolution_subtract_fusion.4
  163.9 0.3 fusion.62
  164.2 0.6 slice-done.1
  164.8 0.6 convolution_subtract_fusion.2
  165.4 11.7 %custom-call.16 = f32[128,128]{1,0:T(8,128)S(1)} custom-call(f32[128,128]{1,0:T(8,128)S(1)} %slice.98), custom_call_target="Cholesky" | custom-call | tf_op jit(solution)/shard_map/cholesky/custom-call.1 | solution.py:42
  177.1 0.7 compare_reduce_fusion.1
  177.8 0.7 select_bitcast_fusion.1
  178.5 9.8 %custom-call.17 = f32[1,128,128]{1,2,0:T(8,128)S(1)} custom-call(f32[1,128,128]{2,1,0:T(8,128)S(1)} %get-tuple-element.14), custom_call_target="InvertDiagBlocksLowerTriangular" | custom-call | tf_op jit(solution)/shard_map/triangular_solve/custom-call.0 | solution.py:43
  188.4 0.3 fusion.30
  188.7 0.3 fusion.47
  189.0 0.7 slice-done
  189.8 0.5 convolution_subtract_fusion.5
  190.3 12.0 %custom-call.18 = f32[128,128]{1,0:T(8,128)S(1)} custom-call(f32[128,128]{1,0:T(8,128)S(1)} %convolution_subtract_fusion.5), custom_call_target="Cholesky" | custom-call | tf_op jit(solution)/shard_map/cholesky/custom-call.1 | solution.py:42
  202.3 0.6 compare_reduce_fusion
  202.9 0.7 select_bitcast_fusion
  203.6 9.8 %custom-call.19 = f32[1,128,128]{1,2,0:T(8,128)S(1)} custom-call(f32[1,128,128]{2,1,0:T(8,128)S(1)} %get-tuple-element.12), custom_call_target="InvertDiagBlocksLowerTriangular" | custom-call | tf_op jit(solution)/shard_map/triangular_solve/custom-call.0 | solution.py:43
  213.4 0.3 fusion.28
  213.7 0.6 convolution_subtract_fusion.3
  214.3 0.3 fusion.63
  214.6 0.8 convolution_subtract_fusion.1
  215.4 0.3 fusion.64
  215.8 1.0 copy.26
  216.9 1.3 copy.27
  (26 shorter events, 0.6 us)
Async XLA Ops:
  115.2 23.2 %copy-start = (f32[256,512]{1,0:T(8,128)S(1)}, f32[256,512]{1,0:T(8,128)}, u32[]{:S(2)}) copy-start(f32[256,512]{1,0:T(8,128)} %param.4) | copy-start | bytes 1572868
  139.1 24.4 %copy-start.1 = (f32[384,128]{0,1:T(8,128)}, f32[384,128]{0,1:T(8,128)S(1)}, u32[]{:S(2)}) copy-start(f32[384,128]{0,1:T(8,128)S(1)} %fusion.21) | copy-start | bytes 589828
  163.3 0.8 copy-start.2
  163.9 0.9 slice-start.1
  188.9 0.8 slice-start
  188.9 0.9 slice-start.2

commit v5 on v4

--- a/solution.py
+++ b/solution.py
@@ -15,27 +15,30 @@
     )
 
 
-def summed(gram):
+def lower_pairs(nb):
+    return [(i, j) for j in range(nb) for i in range(j, nb)]
+
+
+def summed(packed):
     n_rows = lax.axis_size("rows")
     n_chip = lax.axis_size("chip")
-    shape = gram.shape
-    x = gram.reshape(-1, 128)
-    for axis, n in (("rows", n_rows), ("chip", n_chip)):
-        got = lax.all_to_all(x, axis, 0, 0, tiled=True)
-        x = jnp.sum(got.reshape(n, x.shape[0] // n, 128), axis=0)
-    for axis, n in (("chip", n_chip), ("rows", n_rows)):
-        x = lax.all_to_all(jnp.tile(x, (n, 1)), axis, 0, 0, tiled=True)
-    return x.reshape(shape)
+    x = packed
+    got = lax.all_to_all(x, "rows", 0, 0, tiled=True)
+    x = jnp.sum(got.reshape(n_rows, x.shape[0] // n_rows, BLOCK), axis=0)
+    kept = x.shape[0]
+    padded = -(-kept // n_chip) * n_chip
+    x = jnp.pad(x, ((0, padded - kept), (0, 0)))
+    got = lax.all_to_all(x, "chip", 0, 0, tiled=True)
+    x = jnp.sum(got.reshape(n_chip, padded // n_chip, BLOCK), axis=0)
+    x = lax.all_to_all(jnp.tile(x, (n_chip, 1)), "chip", 0, 0, tiled=True)[:kept]
+    return lax.all_to_all(jnp.tile(x, (n_rows, 1)), "rows", 0, 0, tiled=True)
 
 
-def factor(gram):
-    a = (gram + gram.T) / 2
-    n = a.shape[0]
-    nb = n // BLOCK
+def factor(blocks, nb):
     cols, invs = [], []
     for j in range(nb):
-        s = slice(j * BLOCK, (j + 1) * BLOCK)
-        rest = a[j * BLOCK:, s]
+        diag = blocks[(j, j)]
+        rest = jnp.concatenate([(diag + diag.T) / 2] + [blocks[(i, j)] for i in range(j + 1, nb)], axis=0)
         if j:
             done = jnp.concatenate([c[j * BLOCK - k * BLOCK:] for k, c in enumerate(cols)], axis=1)
             rest = rest - mm(done, done[:BLOCK], ((1,), (1,)))
@@ -49,7 +52,7 @@
         cols.append(col)
         invs.append(inv)
     lower = jnp.concatenate(
-        [jnp.concatenate([jnp.zeros((k * BLOCK, BLOCK), a.dtype), c], axis=0) for k, c in enumerate(cols)],
+        [jnp.concatenate([jnp.zeros((k * BLOCK, BLOCK), diag.dtype), c], axis=0) for k, c in enumerate(cols)],
         axis=1,
     )
     return lower, invs
@@ -68,8 +71,15 @@
 
 def on_device(spectra):
     total_rows = lax.axis_size("rows") * lax.axis_size("chip") * spectra.shape[0]
-    gram = summed(mm(spectra, spectra, ((0,), (0,))))
-    lower, invs = factor(gram)
+    nb = spectra.shape[1] // BLOCK
+    pairs = lower_pairs(nb)
+    gram = mm(spectra, spectra, ((0,), (0,)))
+    packed = jnp.concatenate(
+        [gram[i * BLOCK:(i + 1) * BLOCK, j * BLOCK:(j + 1) * BLOCK] for i, j in pairs], axis=0
+    )
+    total = summed(packed)
+    blocks = {p: total[k * BLOCK:(k + 1) * BLOCK] for k, p in enumerate(pairs)}
+    lower, invs = factor(blocks, nb)
     basis = whiten(spectra, lower, invs)
     factor_scale = math.sqrt(total_rows)
     return (basis * factor_scale, lower.T / factor_scale)

time: 221 us -> 211 us (0.955)
  blocking collectives: 111 us -> 100 us
    all_to_all x4, blocking collectives: 111 us -> 100 us  [the longest x1 32.7 us: summed(): got = lax.all_to_all(x, 'rows', 0, 0, tiled=True)]
where the time goes in v5:
time: 211 us; the launch traced here: 208 us
  blocking collectives  100 us (47%)
  other arithmetic  92.2 us (44%)
  matrix products  8.77 us (4%)
  local copies, waits for them, and re-layouts  5.86 us (3%)
    another operation x12, other arithmetic, factor(): diag = lax.linalg.cholesky(rest[:BLOCK], symmetrize_input=False)  49.9 us
    another operation x8, other arithmetic, factor(): lax.linalg.triangular_solve(diag, jnp.eye(BLOCK, dtype=diag.dtype), left_...  42 us
    all_to_all x1, blocking collectives, summed(): got = lax.all_to_all(x, 'rows', 0, 0, tiled=True)  32.7 us
    all_to_all x1, blocking collectives, summed(): got = lax.all_to_all(x, 'chip', 0, 0, tiled=True)  29.5 us
    all_to_all x1, blocking collectives, summed(): return lax.all_to_all(jnp.tile(x, (n_rows, 1)), 'rows', 0, 0, tiled=True)  27.8 us
    all_to_all x1, blocking collectives, summed(): lax.all_to_all(jnp.tile(x, (n_chip, 1)), 'chip', 0, 0, tiled=True)[:kept]  10.2 us
    dot_general x14, matrix products, mm(): lax.dot_general(a, b, (dims, ((), ())), precision=lax.Precision.HIGHEST,...  7.63 us

profile of v5, /device:TPU:1, one launch (start us, length us, event | category | flops | bytes accessed | tf_op | source)
XLA Modules:
  0.0 208.1 jit_solution(3585641255864275455)
XLA Ops:
  0.6 2.2 %fusion.66 = f32[512,512]{1,0:T(8,128)S(1)} fusion(f32[256,512]{1,0:T(8,128)} %param.4), kind=kOutput, calls=%fused_computation.101 | convolution fusion | flops 805306368 | bytes 1572864 | tf_op jit(solution)/shard_map/dot_general | solution.py:13
  3.1 32.7 %all_to_all.33 = f32[64,20,128]{2,1,0:T(8,128)S(1)} all-to-all(f32[64,20,128]{2,1,0:T(8,128)S(1)} %all_to_all.22), channel_id=1, replica_groups=mesh['rows'=64,'chip'=16] {'rows'}, dimensions={0} | all-to-all | bytes 1310720 | tf_op jit(solution)/shard_map/all_to_all | solution.py:26
  35.8 0.1 reduce_sum.18
  35.9 29.5 %all_to_all.34 = f32[16,2,128]{2,1,0:T(2,128)S(1)} all-to-all(f32[16,2,128]{2,1,0:T(2,128)S(1)} %bitcast.59), channel_id=1, replica_groups=mesh['rows'=64,'chip'=16] {'chip'}, dimensions={0} | all-to-all | bytes 32768 | tf_op jit(solution)/shard_map/all_to_all | solution.py:31
  65.4 10.2 %all_to_all.35 = f32[16,2,128]{2,1,0:T(2,128)S(1)} all-to-all(f32[16,2,128]{2,1,0:T(2,128)S(1)} %tile.6), channel_id=1, replica_groups=mesh['rows'=64,'chip'=16] {'chip'}, dimensions={0} | all-to-all | bytes 32768 | tf_op jit(solution)/shard_map/all_to_all | solution.py:33
  75.6 27.8 %all_to_all.36 = f32[64,20,128]{2,1,0:T(8,128)S(1)} all-to-all(f32[64,20,128]{2,1,0:T(8,128)S(1)} %tile.8), channel_id=1, replica_groups=mesh['rows'=64,'chip'=16] {'rows'}, dimensions={0} | all-to-all | bytes 1310720 | tf_op jit(solution)/shard_map/all_to_all | solution.py:34
  103.7 0.1 copy.55
  103.8 0.1 copy.54
  103.9 11.7 %custom-call.12 = f32[128,128]{1,0:T(8,128)S(1)} custom-call(f32[128,128]{1,0:T(8,128)S(1)} %get-tuple-element.21), custom_call_target="Cholesky" | custom-call | tf_op jit(solution)/shard_map/cholesky/custom-call.1 | solution.py:45
  115.7 0.6 compare_reduce_fusion.3
  116.3 0.7 select_bitcast_fusion.3
  117.0 9.8 %custom-call.13 = f32[1,128,128]{1,2,0:T(8,128)S(1)} custom-call(f32[1,128,128]{2,1,0:T(8,128)S(1)} %get-tuple-element.18), custom_call_target="InvertDiagBlocksLowerTriangular" | custom-call | tf_op jit(solution)/shard_map/triangular_solve/custom-call.0 | solution.py:46
  126.8 0.3 fusion.33
  127.1 0.3 fusion.44
  127.4 0.4 fusion.20
  127.8 1.0 slice-done.2
  128.8 0.5 convolution_subtract_fusion
  129.3 11.7 %custom-call.14 = f32[128,128]{1,0:T(8,128)S(1)} custom-call(f32[128,128]{1,0:T(8,128)S(1)} %slice.140), custom_call_target="Cholesky" | custom-call | tf_op jit(solution)/shard_map/cholesky/custom-call.1 | solution.py:45
  141.0 0.7 compare_reduce_fusion.2
  141.7 0.7 select_bitcast_fusion.2
  142.5 10.0 %custom-call.15 = f32[1,128,128]{1,2,0:T(8,128)S(1)} custom-call(f32[1,128,128]{2,1,0:T(8,128)S(1)} %get-tuple-element.16), custom_call_target="InvertDiagBlocksLowerTriangular" | custom-call | tf_op jit(solution)/shard_map/triangular_solve/custom-call.0 | solution.py:46
  152.4 0.3 fusion.31
  152.7 0.3 fusion.42
  153.1 0.1 copy.44
  153.4 0.3 copy-done.5
  153.7 0.5 slice-done.1
  154.2 0.6 convolution_subtract_fusion.2
  154.8 11.7 %custom-call.16 = f32[128,128]{1,0:T(8,128)S(1)} custom-call(f32[128,128]{1,0:T(8,128)S(1)} %slice.145), custom_call_target="Cholesky" | custom-call | tf_op jit(solution)/shard_map/cholesky/custom-call.1 | solution.py:45
  166.5 0.6 compare_reduce_fusion.1
  167.2 0.6 select_bitcast_fusion.1
  167.8 9.8 %custom-call.17 = f32[1,128,128]{1,2,0:T(8,128)S(1)} custom-call(f32[1,128,128]{2,1,0:T(8,128)S(1)} %get-tuple-element.14), custom_call_target="InvertDiagBlocksLowerTriangular" | custom-call | tf_op jit(solution)/shard_map/triangular_solve/custom-call.0 | solution.py:46
  177.6 0.3 fusion.29
  177.9 0.3 fusion.46
  178.2 0.7 slice-done
  179.0 0.5 convolution_subtract_fusion.5
  179.5 12.0 %custom-call.18 = f32[128,128]{1,0:T(8,128)S(1)} custom-call(f32[128,128]{1,0:T(8,128)S(1)} %convolution_subtract_fusion.5), custom_call_target="Cholesky" | custom-call | tf_op jit(solution)/shard_map/cholesky/custom-call.1 | solution.py:45
  191.5 0.6 compare_reduce_fusion
  192.1 0.7 select_bitcast_fusion
  192.8 9.8 %custom-call.19 = f32[1,128,128]{1,2,0:T(8,128)S(1)} custom-call(f32[1,128,128]{2,1,0:T(8,128)S(1)} %get-tuple-element.12), custom_call_target="InvertDiagBlocksLowerTriangular" | custom-call | tf_op jit(solution)/shard_map/triangular_solve/custom-call.0 | solution.py:46
  202.6 0.3 fusion.27
  202.9 0.4 convolution_subtract_fusion.4
  203.3 0.3 fusion.67
  203.6 0.6 convolution_subtract_fusion.3
  204.2 0.3 fusion.68
  204.5 0.8 convolution_subtract_fusion.1
  205.4 0.3 fusion.69
  205.7 1.0 copy.51
  206.8 1.3 copy.52
  (45 shorter events, 1.1 us)
Async XLA Ops:
  103.5 23.8 %copy-start.3 = (f32[1280,128]{1,0:T(8,128)}, f32[1280,128]{1,0:T(8,128)S(1)}, u32[]{:S(2)}) copy-start(f32[1280,128]{1,0:T(8,128)S(1)} %all_to_all.28) | copy-start | bytes 1966084
  103.9 23.2 %copy-start = (f32[256,512]{1,0:T(8,128)S(1)}, f32[256,512]{1,0:T(8,128)}, u32[]{:S(2)}) copy-start(f32[256,512]{1,0:T(8,128)} %param.4) | copy-start | bytes 1572868
  127.8 25.4 %copy-start.1 = (f32[384,128]{0,1:T(8,128)}, f32[384,128]{0,1:T(8,128)S(1)}, u32[]{:S(2)}) copy-start(f32[384,128]{0,1:T(8,128)S(1)} %fusion.20) | copy-start | bytes 589828
  127.8 1.0 slice-start.2
  153.0 0.6 copy-start.5
  153.3 0.9 slice-start.1
  154.2 24.1 %copy-start.4 = (f32[1280,128]{1,0:T(8,128)S(1)}, f32[1280,128]{1,0:T(8,128)}, u32[]{:S(2)}) copy-start(f32[1280,128]{1,0:T(8,128)} %copy-done.3) | copy-start | bytes 1966084
  178.1 0.8 slice-start
  178.1 0.9 slice-start.3
  191.5 11.5 %copy-start.2 = (f32[384,128]{0,1:T(8,128)S(1)}, f32[384,128]{0,1:T(8,128)}, u32[]{:S(2)}) copy-start(f32[384,128]{0,1:T(8,128)} %copy-done.1) | copy-start | bytes 589828

commit v6 on v5

--- a/solution.py
+++ b/solution.py
@@ -25,12 +25,8 @@
     x = packed
     got = lax.all_to_all(x, "rows", 0, 0, tiled=True)
     x = jnp.sum(got.reshape(n_rows, x.shape[0] // n_rows, BLOCK), axis=0)
-    kept = x.shape[0]
-    padded = -(-kept // n_chip) * n_chip
-    x = jnp.pad(x, ((0, padded - kept), (0, 0)))
-    got = lax.all_to_all(x, "chip", 0, 0, tiled=True)
-    x = jnp.sum(got.reshape(n_chip, padded // n_chip, BLOCK), axis=0)
-    x = lax.all_to_all(jnp.tile(x, (n_chip, 1)), "chip", 0, 0, tiled=True)[:kept]
+    got = lax.all_to_all(jnp.tile(x, (n_chip, 1)), "chip", 0, 0, tiled=True)
+    x = jnp.sum(got.reshape(n_chip, x.shape[0], BLOCK), axis=0)
     return lax.all_to_all(jnp.tile(x, (n_rows, 1)), "rows", 0, 0, tiled=True)
 
 

time: 211 us -> 204 us (0.967)
  blocking collectives: 100 us -> 94.2 us
    all_to_all x2 -> x1, blocking collectives: 39.6 us -> 32.3 us  [summed(): got = lax.all_to_all(jnp.tile(x, (n_chip, 1)), 'chip', 0, 0, tiled=True)]
where the time goes in v6:
time: 204 us; the launch traced here: 202 us
  blocking collectives  94.2 us (46%)
  other arithmetic  92.2 us (45%)
  matrix products  8.77 us (4%)
  local copies, waits for them, and re-layouts  5.84 us (3%)
    another operation x12, other arithmetic, factor(): diag = lax.linalg.cholesky(rest[:BLOCK], symmetrize_input=False)  49.9 us
    another operation x8, other arithmetic, factor(): lax.linalg.triangular_solve(diag, jnp.eye(BLOCK, dtype=diag.dtype), left_...  42 us
    all_to_all x1, blocking collectives, summed(): got = lax.all_to_all(x, 'rows', 0, 0, tiled=True)  32.7 us
    all_to_all x1, blocking collectives, summed(): got = lax.all_to_all(jnp.tile(x, (n_chip, 1)), 'chip', 0, 0, tiled=True)  32.3 us
    all_to_all x1, blocking collectives, summed(): return lax.all_to_all(jnp.tile(x, (n_rows, 1)), 'rows', 0, 0, tiled=True)  29.1 us
    dot_general x14, matrix products, mm(): lax.dot_general(a, b, (dims, ((), ())), precision=lax.Precision.HIGHEST,...  7.63 us

profile of v6, /device:TPU:1, one launch (start us, length us, event | category | flops | bytes accessed | tf_op | source)
XLA Modules:
  0.0 202.1 jit_solution(10341138014639794587)
XLA Ops:
  0.6 2.2 %fusion.66 = f32[512,512]{1,0:T(8,128)S(1)} fusion(f32[256,512]{1,0:T(8,128)} %param.4), kind=kOutput, calls=%fused_computation.101 | convolution fusion | flops 805306368 | bytes 1572864 | tf_op jit(solution)/shard_map/dot_general | solution.py:13
  3.1 32.7 %all_to_all.24 = f32[64,20,128]{2,1,0:T(8,128)S(1)} all-to-all(f32[64,20,128]{2,1,0:T(8,128)S(1)} %all_to_all.16), channel_id=1, replica_groups=mesh['rows'=64,'chip'=16] {'rows'}, dimensions={0} | all-to-all | bytes 1310720 | tf_op jit(solution)/shard_map/all_to_all | solution.py:26
  35.8 0.1 reduce_sum.18
  35.9 32.3 %all_to_all.25 = f32[16,20,128]{2,1,0:T(8,128)S(1)} all-to-all(f32[16,20,128]{2,1,0:T(8,128)S(1)} %tile.4), channel_id=1, replica_groups=mesh['rows'=64,'chip'=16] {'chip'}, dimensions={0} | all-to-all | bytes 327680 | tf_op jit(solution)/shard_map/all_to_all | solution.py:28
  68.3 29.1 %all_to_all.26 = f32[64,20,128]{2,1,0:T(8,128)S(1)} all-to-all(f32[64,20,128]{2,1,0:T(8,128)S(1)} %tile.5), channel_id=1, replica_groups=mesh['rows'=64,'chip'=16] {'rows'}, dimensions={0} | all-to-all | bytes 1310720 | tf_op jit(solution)/shard_map/all_to_all | solution.py:30
  97.6 0.1 copy.55
  97.7 0.1 copy.54
  97.9 11.7 %custom-call.12 = f32[128,128]{1,0:T(8,128)S(1)} custom-call(f32[128,128]{1,0:T(8,128)S(1)} %get-tuple-element.21), custom_call_target="Cholesky" | custom-call | tf_op jit(solution)/shard_map/cholesky/custom-call.1 | solution.py:41
  109.7 0.6 compare_reduce_fusion.3
  110.3 0.7 select_bitcast_fusion.3
  111.0 9.8 %custom-call.13 = f32[1,128,128]{1,2,0:T(8,128)S(1)} custom-call(f32[1,128,128]{2,1,0:T(8,128)S(1)} %get-tuple-element.18), custom_call_target="InvertDiagBlocksLowerTriangular" | custom-call | tf_op jit(solution)/shard_map/triangular_solve/custom-call.0 | solution.py:42
  120.8 0.3 fusion.33
  121.1 0.3 fusion.44
  121.4 0.4 fusion.20
  121.8 1.0 slice-done.2
  122.8 0.5 convolution_subtract_fusion
  123.3 11.7 %custom-call.14 = f32[128,128]{1,0:T(8,128)S(1)} custom-call(f32[128,128]{1,0:T(8,128)S(1)} %slice.134), custom_call_target="Cholesky" | custom-call | tf_op jit(solution)/shard_map/cholesky/custom-call.1 | solution.py:41
  135.0 0.7 compare_reduce_fusion.2
  135.7 0.7 select_bitcast_fusion.2
  136.4 10.0 %custom-call.15 = f32[1,128,128]{1,2,0:T(8,128)S(1)} custom-call(f32[1,128,128]{2,1,0:T(8,128)S(1)} %get-tuple-element.16), custom_call_target="InvertDiagBlocksLowerTriangular" | custom-call | tf_op jit(solution)/shard_map/triangular_solve/custom-call.0 | solution.py:42
  146.4 0.3 fusion.31
  146.7 0.3 fusion.42
  147.1 0.1 copy.44
  147.3 0.1 copy.57
  147.4 0.3 copy-done.5
  147.6 0.5 slice-done.1
  148.2 0.6 convolution_subtract_fusion.2
  148.8 11.7 %custom-call.16 = f32[128,128]{1,0:T(8,128)S(1)} custom-call(f32[128,128]{1,0:T(8,128)S(1)} %slice.139), custom_call_target="Cholesky" | custom-call | tf_op jit(solution)/shard_map/cholesky/custom-call.1 | solution.py:41
  160.5 0.6 compare_reduce_fusion.1
  161.2 0.6 select_bitcast_fusion.1
  161.7 9.8 %custom-call.17 = f32[1,128,128]{1,2,0:T(8,128)S(1)} custom-call(f32[1,128,128]{2,1,0:T(8,128)S(1)} %get-tuple-element.14), custom_call_target="InvertDiagBlocksLowerTriangular" | custom-call | tf_op jit(solution)/shard_map/triangular_solve/custom-call.0 | solution.py:42
  171.6 0.3 fusion.29
  171.8 0.3 fusion.46
  172.2 0.7 slice-done
  173.0 0.5 convolution_subtract_fusion.5
  173.5 12.0 %custom-call.18 = f32[128,128]{1,0:T(8,128)S(1)} custom-call(f32[128,128]{1,0:T(8,128)S(1)} %convolution_subtract_fusion.5), custom_call_target="Cholesky" | custom-call | tf_op jit(solution)/shard_map/cholesky/custom-call.1 | solution.py:41
  185.5 0.6 compare_reduce_fusion
  186.1 0.7 select_bitcast_fusion
  186.8 9.8 %custom-call.19 = f32[1,128,128]{1,2,0:T(8,128)S(1)} custom-call(f32[1,128,128]{2,1,0:T(8,128)S(1)} %get-tuple-element.12), custom_call_target="InvertDiagBlocksLowerTriangular" | custom-call | tf_op jit(solution)/shard_map/triangular_solve/custom-call.0 | solution.py:42
  196.6 0.3 fusion.27
  196.9 0.4 convolution_subtract_fusion.4
  197.3 0.3 fusion.67
  197.6 0.6 convolution_subtract_fusion.3
  198.2 0.3 fusion.68
  198.5 0.8 convolution_subtract_fusion.1
  199.3 0.3 fusion.69
  199.7 1.0 copy.51
  200.8 1.3 copy.52
  (41 shorter events, 1.0 us)
Async XLA Ops:
  97.5 23.8 %copy-start.3 = (f32[1280,128]{1,0:T(8,128)}, f32[1280,128]{1,0:T(8,128)S(1)}, u32[]{:S(2)}) copy-start(f32[1280,128]{1,0:T(8,128)S(1)} %all_to_all.20) | copy-start | bytes 1966084
  97.8 23.2 %copy-start = (f32[256,512]{1,0:T(8,128)S(1)}, f32[256,512]{1,0:T(8,128)}, u32[]{:S(2)}) copy-start(f32[256,512]{1,0:T(8,128)} %param.4) | copy-start | bytes 1572868
  121.8 25.4 %copy-start.1 = (f32[384,128]{0,1:T(8,128)}, f32[384,128]{0,1:T(8,128)S(1)}, u32[]{:S(2)}) copy-start(f32[384,128]{0,1:T(8,128)S(1)} %fusion.20) | copy-start | bytes 589828
  121.8 1.0 slice-start.2
  147.0 0.6 copy-start.5
  147.3 0.9 slice-start.1
  148.2 24.1 %copy-start.4 = (f32[1280,128]{1,0:T(8,128)S(1)}, f32[1280,128]{1,0:T(8,128)}, u32[]{:S(2)}) copy-start(f32[1280,128]{1,0:T(8,128)} %copy-done.3) | copy-start | bytes 1966084
  172.1 0.8 slice-start
  172.1 0.9 slice-start.3
  185.4 11.5 %copy-start.2 = (f32[384,128]{0,1:T(8,128)S(1)}, f32[384,128]{0,1:T(8,128)}, u32[]{:S(2)}) copy-start(f32[384,128]{0,1:T(8,128)} %copy-done.1) | copy-start | bytes 589828

commit v7 on v6

--- a/solution.py
+++ b/solution.py
@@ -65,16 +65,44 @@
     return jnp.concatenate(outs, axis=1)
 
 
+def pack(gram, nb, n_rows):
+    blk = lambda i, j: gram[i * BLOCK:(i + 1) * BLOCK, j * BLOCK:(j + 1) * BLOCK]
+    parts = [blk(i, j) for j in range(nb) for i in range(j + 1, nb)]
+    eye = jnp.eye(BLOCK, dtype=bool)
+    low = jnp.tril(jnp.ones((BLOCK, BLOCK), dtype=bool))
+    for j in range(0, nb, 2):
+        parts.append(jnp.where(low, blk(j, j), blk(j + 1, j + 1)))
+    for j in range(0, nb, 2):
+        parts.append(jnp.diagonal(blk(j + 1, j + 1))[None, :])
+    packed = jnp.concatenate(parts, axis=0)
+    rows = packed.shape[0]
+    return jnp.pad(packed, ((0, -(-rows // n_rows) * n_rows - rows), (0, 0)))
+
+
+def unpack(total, nb):
+    blocks, k = {}, 0
+    for j in range(nb):
+        for i in range(j + 1, nb):
+            blocks[(i, j)] = total[k * BLOCK:(k + 1) * BLOCK]
+            k += 1
+    low = jnp.tril(jnp.ones((BLOCK, BLOCK), dtype=bool))
+    strict = jnp.tril(jnp.ones((BLOCK, BLOCK), dtype=bool), -1)
+    base = k * BLOCK + (nb // 2) * BLOCK
+    for n, j in enumerate(range(0, nb, 2)):
+        both = total[(k + n) * BLOCK:(k + n + 1) * BLOCK]
+        lower = jnp.where(low, both, 0.0)
+        blocks[(j, j)] = lower + jnp.where(strict, both, 0.0).T
+        upper = jnp.where(strict.T, both, 0.0)
+        blocks[(j + 1, j + 1)] = upper + upper.T + jnp.diag(total[base + n])
+    return blocks
+
+
 def on_device(spectra):
     total_rows = lax.axis_size("rows") * lax.axis_size("chip") * spectra.shape[0]
     nb = spectra.shape[1] // BLOCK
-    pairs = lower_pairs(nb)
+    assert nb % 2 == 0
     gram = mm(spectra, spectra, ((0,), (0,)))
-    packed = jnp.concatenate(
-        [gram[i * BLOCK:(i + 1) * BLOCK, j * BLOCK:(j + 1) * BLOCK] for i, j in pairs], axis=0
-    )
-    total = summed(packed)
-    blocks = {p: total[k * BLOCK:(k + 1) * BLOCK] for k, p in enumerate(pairs)}
+    blocks = unpack(summed(pack(gram, nb, lax.axis_size("rows"))), nb)
     lower, invs = factor(blocks, nb)
     basis = whiten(spectra, lower, invs)
     factor_scale = math.sqrt(total_rows)

time: 204 us -> 210 us (1.029)
  blocking collectives: 94.2 us -> 65 us
  waiting for transfers between devices: 0 us -> 22.5 us
  starting transfers between devices: 0 us -> 6.67 us
  local copies, waits for them, and re-layouts: 5.84 us -> 11.6 us
    all_to_all x1 -> x0, blocking collectives: 29.1 us -> none  [summed(): return lax.all_to_all(jnp.tile(x, (n_rows, 1)), 'rows', 0, 0, tiled=True)]
    all_to_all x0 -> x1, waiting for transfers between devices: none -> 22.5 us  [summed(): return lax.all_to_all(jnp.tile(x, (n_rows, 1)), 'rows', 0, 0, tiled=True)]
    all_to_all x0 -> x1, starting transfers between devices: none -> 6.67 us  [summed(): return lax.all_to_all(jnp.tile(x, (n_rows, 1)), 'rows', 0, 0, tiled=True)]
    gather x0 -> x2, local copies, waits for them, and re-layouts: none -> 2.57 us  [pack(): parts.append(jnp.diagonal(blk(j + 1, j + 1))[None, :])]
  transfers between devices with their start and end apart: 0 -> 1, of which waited for: 0 -> 1; matrix products, arithmetic and copies ran while one was open for 0% -> 0% of each run, Pallas kernels for 0% -> 0%
where the time goes in v7:
time: 210 us; the launch traced here: 208 us
  other arithmetic  92.5 us (44%)
  blocking collectives  65 us (31%)
  waiting for transfers between devices  22.5 us (11%)
  local copies, waits for them, and re-layouts  11.6 us (6%)
  matrix products  8.78 us (4%)
  starting transfers between devices  6.67 us (3%)
    another operation x12, other arithmetic, factor(): diag = lax.linalg.cholesky(rest[:BLOCK], symmetrize_input=False)  49.8 us
    another operation x8, other arithmetic, factor(): lax.linalg.triangular_solve(diag, jnp.eye(BLOCK, dtype=diag.dtype), left_...  42.1 us
    all_to_all x1, blocking collectives, summed(): got = lax.all_to_all(x, 'rows', 0, 0, tiled=True)  32.7 us
    all_to_all x1, blocking collectives, summed(): got = lax.all_to_all(jnp.tile(x, (n_chip, 1)), 'chip', 0, 0, tiled=True)  32.3 us
    all_to_all x1, waiting for transfers between devices, summed(): return lax.all_to_all(jnp.tile(x, (n_rows, 1)), 'rows', 0, 0, tiled=True)  22.5 us
    dot_general x14, matrix products, mm(): lax.dot_general(a, b, (dims, ((), ())), precision=lax.Precision.HIGHEST,...  7.64 us
    all_to_all x1, starting transfers between devices, summed(): return lax.all_to_all(jnp.tile(x, (n_rows, 1)), 'rows', 0, 0, tiled=True)  6.67 us
  transfers between devices with their start and end apart: 1, of which 1 were waited for; matrix products, arithmetic and copies ran while one was open for 0% of the time, Pallas kernels for 0%

profile of v7, /device:TPU:1, one launch (start us, length us, event | category | flops | bytes accessed | tf_op | source)
XLA Modules:
  0.0 208.4 jit_solution(4308770462791750820)
XLA Ops:
  0.6 2.2 %fusion.71 = f32[512,512]{1,0:T(8,128)S(1)} fusion(f32[256,512]{1,0:T(8,128)} %param.4), kind=kOutput, calls=%fused_computation.120 | convolution fusion | flops 805306368 | bytes 1572864 | tf_op jit(solution)/shard_map/dot_general | solution.py:13
  3.2 1.3 gather_fusion.1
  4.5 1.3 gather_fusion
  6.3 32.7 %all_to_all.24 = f32[64,17,128]{2,1,0:T(8,128)S(1)} all-to-all(f32[64,17,128]{2,1,0:T(8,128)S(1)} %all_to_all.16), channel_id=1, replica_groups=mesh['rows'=64,'chip'=16] {'rows'}, dimensions={0} | all-to-all | bytes 1114112 | tf_op jit(solution)/shard_map/all_to_all | solution.py:26
  39.2 32.3 %all_to_all.25 = f32[16,17,128]{2,1,0:T(8,128)S(1)} all-to-all(f32[16,17,128]{2,1,0:T(8,128)S(1)} %tile.4), channel_id=1, replica_groups=mesh['rows'=64,'chip'=16] {'chip'}, dimensions={0} | all-to-all | bytes 278528 | tf_op jit(solution)/shard_map/all_to_all | solution.py:28
  71.5 0.9 tile.5
  72.4 6.7 %all-to-all-start.2 = ((f32[64,17,128]{2,1,0:T(8,128)}), f32[64,17,128]{2,1,0:T(8,128)S(1)}, u32[]{:S(2)}, u32[]{:S(2)}) async-start(f32[64,17,128]{2,1,0:T(8,128)} %tile.5), calls=%async_computation.2 | async-start | bytes 1572864 | tf_op jit(solution)/shard_map/all_to_all | solution.py:30
  79.3 22.5 %all-to-all-done.2 = f32[64,17,128]{2,1,0:T(8,128)S(1)} async-done(((f32[64,17,128]{2,1,0:T(8,128)}), f32[64,17,128]{2,1,0:T(8,128)S(1)}, u32[]{:S(2)}, u32[]{:S(2)}) %all-to-all-start.2) | async-done | bytes 557088 | tf_op jit(solution)/shard_map/all_to_all | solution.py:30
  102.4 11.7 %custom-call.16 = f32[128,128]{1,0:T(8,128)S(1)} custom-call(f32[128,128]{1,0:T(8,128)S(1)} %copy.114), custom_call_target="Cholesky" | custom-call | tf_op jit(solution)/shard_map/cholesky/custom-call.1 | solution.py:41
  114.2 0.6 compare_reduce_fusion.3
  114.8 0.7 select_bitcast_fusion.3
  115.5 9.8 %custom-call.17 = f32[1,128,128]{1,2,0:T(8,128)S(1)} custom-call(f32[1,128,128]{2,1,0:T(8,128)S(1)} %get-tuple-element.18), custom_call_target="InvertDiagBlocksLowerTriangular" | custom-call | tf_op jit(solution)/shard_map/triangular_solve/custom-call.0 | solution.py:42
  125.3 0.3 fusion.33
  125.6 0.4 fusion.20
  126.0 0.3 fusion.44
  126.7 0.9 slice-done.3
  127.6 0.5 convolution_subtract_fusion
  128.1 11.7 %custom-call.18 = f32[128,128]{1,0:T(8,128)S(1)} custom-call(f32[128,128]{1,0:T(8,128)S(1)} %slice.151), custom_call_target="Cholesky" | custom-call | tf_op jit(solution)/shard_map/cholesky/custom-call.1 | solution.py:41
  140.0 0.6 compare_reduce_fusion.2
  140.6 0.7 select_bitcast_fusion.2
  141.4 10.0 %custom-call.19 = f32[1,128,128]{1,2,0:T(8,128)S(1)} custom-call(f32[1,128,128]{2,1,0:T(8,128)S(1)} %copy.120), custom_call_target="InvertDiagBlocksLowerTriangular" | custom-call | tf_op jit(solution)/shard_map/triangular_solve/custom-call.0 | solution.py:42
  151.3 0.3 fusion.31
  151.6 0.3 fusion.42
  152.3 0.3 copy-done.3
  152.6 0.6 slice-done.1
  153.2 0.6 convolution_subtract_fusion.2
  153.8 11.7 %custom-call.20 = f32[128,128]{1,0:T(8,128)S(1)} custom-call(f32[128,128]{1,0:T(8,128)S(1)} %slice.156), custom_call_target="Cholesky" | custom-call | tf_op jit(solution)/shard_map/cholesky/custom-call.1 | solution.py:41
  165.9 0.6 copy-done.2
  166.5 0.4 convolution_subtract_fusion.4
  166.9 0.3 fusion.72
  167.2 0.7 compare_reduce_fusion.1
  167.9 0.7 select_bitcast_fusion.1
  168.7 9.8 %custom-call.21 = f32[1,128,128]{1,2,0:T(8,128)S(1)} custom-call(f32[1,128,128]{2,1,0:T(8,128)S(1)} %copy.129), custom_call_target="InvertDiagBlocksLowerTriangular" | custom-call | tf_op jit(solution)/shard_map/triangular_solve/custom-call.0 | solution.py:42
  178.5 0.3 fusion.29
  178.8 0.3 fusion.46
  179.3 0.7 slice-done
  180.0 0.5 convolution_subtract_fusion.5
  180.5 11.9 %custom-call.22 = f32[128,128]{1,0:T(8,128)S(1)} custom-call(f32[128,128]{1,0:T(8,128)S(1)} %convolution_subtract_fusion.5), custom_call_target="Cholesky" | custom-call | tf_op jit(solution)/shard_map/cholesky/custom-call.1 | solution.py:41
  192.5 0.6 compare_reduce_fusion
  193.1 0.7 select_bitcast_fusion
  193.8 9.8 %custom-call.23 = f32[1,128,128]{1,2,0:T(8,128)S(1)} custom-call(f32[1,128,128]{2,1,0:T(8,128)S(1)} %get-tuple-element.12), custom_call_target="InvertDiagBlocksLowerTriangular" | custom-call | tf_op jit(solution)/shard_map/triangular_solve/custom-call.0 | solution.py:42
  203.6 0.3 fusion.27
  203.9 0.6 convolution_subtract_fusion.3
  204.5 0.3 fusion.73
  204.8 0.8 convolution_subtract_fusion.1
  205.7 0.3 fusion.74
  206.0 1.0 copy.135
  207.1 1.3 copy.136
  (70 shorter events, 3.4 us)
Async XLA Ops:
  72.4 29.3 %all-to-all-start.2 = ((f32[64,17,128]{2,1,0:T(8,128)}), f32[64,17,128]{2,1,0:T(8,128)S(1)}, u32[]{:S(2)}, u32[]{:S(2)}) async-start(f32[64,17,128]{2,1,0:T(8,128)} %tile.5), calls=%async_computation.2 | async-start | bytes 1572864 | tf_op jit(solution)/shard_map/all_to_all | solution.py:30
  101.8 23.7 %copy-start.4 = (f32[1088,128]{1,0:T(8,128)}, f32[1088,128]{1,0:T(8,128)S(1)}, u32[]{:S(2)}) copy-start(f32[1088,128]{1,0:T(8,128)S(1)} %all_to_all.20) | copy-start | bytes 1671172
  102.3 23.7 %copy-start = (f32[256,512]{1,0:T(8,128)S(1)}, f32[256,512]{1,0:T(8,128)}, u32[]{:S(2)}) copy-start(f32[256,512]{1,0:T(8,128)} %param.4) | copy-start | bytes 1572868
  126.0 26.0 %copy-start.1 = (f32[384,128]{0,1:T(8,128)}, f32[384,128]{0,1:T(8,128)S(1)}, u32[]{:S(2)}) copy-start(f32[384,128]{0,1:T(8,128)S(1)} %fusion.20) | copy-start | bytes 589828
  126.7 0.9 slice-start.3
  151.9 0.7 copy-start.3
  152.3 0.9 slice-start.1
  165.5 0.9 copy-start.2
  179.2 0.8 slice-start
  179.2 0.9 slice-start.2

commit v8 on v6

--- a/solution.py
+++ b/solution.py
@@ -69,9 +69,9 @@
     total_rows = lax.axis_size("rows") * lax.axis_size("chip") * spectra.shape[0]
     nb = spectra.shape[1] // BLOCK
     pairs = lower_pairs(nb)
-    gram = mm(spectra, spectra, ((0,), (0,)))
     packed = jnp.concatenate(
-        [gram[i * BLOCK:(i + 1) * BLOCK, j * BLOCK:(j + 1) * BLOCK] for i, j in pairs], axis=0
+        [mm(spectra[:, j * BLOCK:], spectra[:, j * BLOCK:(j + 1) * BLOCK], ((0,), (0,))) for j in range(nb)],
+        axis=0,
     )
     total = summed(packed)
     blocks = {p: total[k * BLOCK:(k + 1) * BLOCK] for k, p in enumerate(pairs)}

time: 204 us -> 206 us (level)
  matrix products: 8.77 us -> 11.3 us
    dot_general x14 -> x17, matrix products: 7.63 us -> 10.2 us  [mm(): lax.dot_general(a, b, (dims, ((), ())), precision=lax.Precision.HIGHEST,...]
where the time goes in v8:
time: 206 us; the launch traced here: 204 us
  blocking collectives  94.2 us (46%)
  other arithmetic  92.1 us (45%)
  matrix products  11.3 us (5%)
  local copies, waits for them, and re-layouts  5.75 us (3%)
    another operation x12, other arithmetic, factor(): diag = lax.linalg.cholesky(rest[:BLOCK], symmetrize_input=False)  49.8 us
    another operation x8, other arithmetic, factor(): lax.linalg.triangular_solve(diag, jnp.eye(BLOCK, dtype=diag.dtype), left_...  42 us
    all_to_all x1, blocking collectives, summed(): got = lax.all_to_all(x, 'rows', 0, 0, tiled=True)  32.7 us
    all_to_all x1, blocking collectives, summed(): got = lax.all_to_all(jnp.tile(x, (n_chip, 1)), 'chip', 0, 0, tiled=True)  32.3 us
    all_to_all x1, blocking collectives, summed(): return lax.all_to_all(jnp.tile(x, (n_rows, 1)), 'rows', 0, 0, tiled=True)  29.1 us
    dot_general x17, matrix products, mm(): lax.dot_general(a, b, (dims, ((), ())), precision=lax.Precision.HIGHEST,...  10.2 us

profile of v8, /device:TPU:1, one launch (start us, length us, event | category | flops | bytes accessed | tf_op | source)
XLA Modules:
  0.0 204.5 jit_solution(2408488465599264045)
XLA Ops:
  0.6 1.4 fusion.48
  2.1 1.6 fusion.15
  3.7 0.8 fusion.7
  4.5 1.0 fusion.54
  5.6 32.7 %all_to_all.24 = f32[64,20,128]{2,1,0:T(8,128)S(1)} all-to-all(f32[64,20,128]{2,1,0:T(8,128)S(1)} %all_to_all.16), channel_id=1, replica_groups=mesh['rows'=64,'chip'=16] {'rows'}, dimensions={0} | all-to-all | bytes 1310720 | tf_op jit(solution)/shard_map/all_to_all | solution.py:26
  38.4 32.3 %all_to_all.25 = f32[16,20,128]{2,1,0:T(8,128)S(1)} all-to-all(f32[16,20,128]{2,1,0:T(8,128)S(1)} %tile.4), channel_id=1, replica_groups=mesh['rows'=64,'chip'=16] {'chip'}, dimensions={0} | all-to-all | bytes 327680 | tf_op jit(solution)/shard_map/all_to_all | solution.py:28
  70.8 29.1 %all_to_all.26 = f32[64,20,128]{2,1,0:T(8,128)S(1)} all-to-all(f32[64,20,128]{2,1,0:T(8,128)S(1)} %tile.5), channel_id=1, replica_groups=mesh['rows'=64,'chip'=16] {'rows'}, dimensions={0} | all-to-all | bytes 1310720 | tf_op jit(solution)/shard_map/all_to_all | solution.py:30
  100.1 0.1 copy.55
  100.4 11.7 %custom-call.12 = f32[128,128]{1,0:T(8,128)S(1)} custom-call(f32[128,128]{1,0:T(8,128)S(1)} %get-tuple-element.21), custom_call_target="Cholesky" | custom-call | tf_op jit(solution)/shard_map/cholesky/custom-call.1 | solution.py:41
  112.1 0.6 compare_reduce_fusion.3
  112.8 0.7 select_bitcast_fusion.3
  113.4 9.8 %custom-call.13 = f32[1,128,128]{1,2,0:T(8,128)S(1)} custom-call(f32[1,128,128]{2,1,0:T(8,128)S(1)} %get-tuple-element.18), custom_call_target="InvertDiagBlocksLowerTriangular" | custom-call | tf_op jit(solution)/shard_map/triangular_solve/custom-call.0 | solution.py:42
  123.2 0.3 fusion.37
  123.5 0.3 fusion.52
  123.8 0.4 fusion.24
  124.2 1.0 slice-done.2
  125.2 0.5 convolution_subtract_fusion
  125.7 11.7 %custom-call.14 = f32[128,128]{1,0:T(8,128)S(1)} custom-call(f32[128,128]{1,0:T(8,128)S(1)} %slice.118), custom_call_target="Cholesky" | custom-call | tf_op jit(solution)/shard_map/cholesky/custom-call.1 | solution.py:41
  137.5 0.7 compare_reduce_fusion.2
  138.2 0.7 select_bitcast_fusion.2
  138.9 10.0 %custom-call.15 = f32[1,128,128]{1,2,0:T(8,128)S(1)} custom-call(f32[1,128,128]{2,1,0:T(8,128)S(1)} %get-tuple-element.16), custom_call_target="InvertDiagBlocksLowerTriangular" | custom-call | tf_op jit(solution)/shard_map/triangular_solve/custom-call.0 | solution.py:42
  148.9 0.3 fusion.35
  149.2 0.3 fusion.46
  149.6 0.1 copy.44
  149.8 0.3 copy-done.5
  150.1 0.5 slice-done.1
  150.6 0.6 convolution_subtract_fusion.2
  151.2 11.7 %custom-call.16 = f32[128,128]{1,0:T(8,128)S(1)} custom-call(f32[128,128]{1,0:T(8,128)S(1)} %slice.123), custom_call_target="Cholesky" | custom-call | tf_op jit(solution)/shard_map/cholesky/custom-call.1 | solution.py:41
  163.0 0.6 compare_reduce_fusion.1
  163.6 0.6 select_bitcast_fusion.1
  164.2 9.8 %custom-call.17 = f32[1,128,128]{1,2,0:T(8,128)S(1)} custom-call(f32[1,128,128]{2,1,0:T(8,128)S(1)} %get-tuple-element.14), custom_call_target="InvertDiagBlocksLowerTriangular" | custom-call | tf_op jit(solution)/shard_map/triangular_solve/custom-call.0 | solution.py:42
  174.0 0.3 fusion.33
  174.3 0.3 fusion.56
  174.7 0.7 slice-done
  175.5 0.5 convolution_subtract_fusion.5
  176.0 11.9 %custom-call.18 = f32[128,128]{1,0:T(8,128)S(1)} custom-call(f32[128,128]{1,0:T(8,128)S(1)} %convolution_subtract_fusion.5), custom_call_target="Cholesky" | custom-call | tf_op jit(solution)/shard_map/cholesky/custom-call.1 | solution.py:41
  187.9 0.6 compare_reduce_fusion
  188.6 0.7 select_bitcast_fusion
  189.2 9.8 %custom-call.19 = f32[1,128,128]{1,2,0:T(8,128)S(1)} custom-call(f32[1,128,128]{2,1,0:T(8,128)S(1)} %get-tuple-element.12), custom_call_target="InvertDiagBlocksLowerTriangular" | custom-call | tf_op jit(solution)/shard_map/triangular_solve/custom-call.0 | solution.py:42
  199.0 0.3 fusion.31
  199.3 0.4 convolution_subtract_fusion.4
  199.7 0.3 fusion.76
  200.0 0.6 convolution_subtract_fusion.3
  200.6 0.3 fusion.77
  200.9 0.8 convolution_subtract_fusion.1
  201.8 0.3 fusion.78
  202.1 1.0 copy.51
  203.2 1.3 copy.52
  (40 shorter events, 1.2 us)
Async XLA Ops:
  0.6 3.0 %copy-start = (f32[256,512]{1,0:T(8,128)S(1)}, f32[256,512]{1,0:T(8,128)}, u32[]{:S(2)}) copy-start(f32[256,512]{1,0:T(8,128)} %param.4) | copy-start | bytes 1572868
  100.0 23.8 %copy-start.3 = (f32[1280,128]{1,0:T(8,128)}, f32[1280,128]{1,0:T(8,128)S(1)}, u32[]{:S(2)}) copy-start(f32[1280,128]{1,0:T(8,128)S(1)} %all_to_all.20) | copy-start | bytes 1966084
  124.2 25.4 %copy-start.1 = (f32[384,128]{0,1:T(8,128)}, f32[384,128]{0,1:T(8,128)S(1)}, u32[]{:S(2)}) copy-start(f32[384,128]{0,1:T(8,128)S(1)} %fusion.24) | copy-start | bytes 589828
  124.2 1.0 slice-start.2
  149.5 0.6 copy-start.5
  149.7 0.9 slice-start.1
  150.6 24.1 %copy-start.4 = (f32[1280,128]{1,0:T(8,128)S(1)}, f32[1280,128]{1,0:T(8,128)}, u32[]{:S(2)}) copy-start(f32[1280,128]{1,0:T(8,128)} %copy-done.3) | copy-start | bytes 1966084
  174.6 0.8 slice-start
  174.6 0.9 slice-start.3
  187.9 11.5 %copy-start.2 = (f32[384,128]{0,1:T(8,128)S(1)}, f32[384,128]{0,1:T(8,128)}, u32[]{:S(2)}) copy-start(f32[384,128]{0,1:T(8,128)} %copy-done.1) | copy-start | bytes 589828

commit v9 on v6

--- a/solution.py
+++ b/solution.py
@@ -34,7 +34,7 @@
     cols, invs = [], []
     for j in range(nb):
         diag = blocks[(j, j)]
-        rest = jnp.concatenate([(diag + diag.T) / 2] + [blocks[(i, j)] for i in range(j + 1, nb)], axis=0)
+        rest = jnp.concatenate([diag] + [blocks[(i, j)] for i in range(j + 1, nb)], axis=0)
         if j:
             done = jnp.concatenate([c[j * BLOCK - k * BLOCK:] for k, c in enumerate(cols)], axis=1)
             rest = rest - mm(done, done[:BLOCK], ((1,), (1,)))

time: 204 us -> 202 us (level)
  no operation moved by 1% of the time
where the time goes in v9:
time: 202 us; the launch traced here: 201 us
  blocking collectives  94.2 us (47%)
  other arithmetic  92.2 us (46%)
  matrix products  8.78 us (4%)
  local copies, waits for them, and re-layouts  4.3 us (2%)
    another operation x12, other arithmetic, factor(): diag = lax.linalg.cholesky(rest[:BLOCK], symmetrize_input=False)  49.9 us
    another operation x8, other arithmetic, factor(): lax.linalg.triangular_solve(diag, jnp.eye(BLOCK, dtype=diag.dtype), left_...  42.1 us
    all_to_all x1, blocking collectives, summed(): got = lax.all_to_all(x, 'rows', 0, 0, tiled=True)  32.7 us
    all_to_all x1, blocking collectives, summed(): got = lax.all_to_all(jnp.tile(x, (n_chip, 1)), 'chip', 0, 0, tiled=True)  32.3 us
    all_to_all x1, blocking collectives, summed(): return lax.all_to_all(jnp.tile(x, (n_rows, 1)), 'rows', 0, 0, tiled=True)  29.1 us
    dot_general x14, matrix products, mm(): lax.dot_general(a, b, (dims, ((), ())), precision=lax.Precision.HIGHEST,...  7.64 us

profile of v9, /device:TPU:1, one launch (start us, length us, event | category | flops | bytes accessed | tf_op | source)
XLA Modules:
  0.0 200.5 jit_solution(14619009033386392482)
XLA Ops:
  0.6 2.2 %fusion.60 = f32[512,512]{1,0:T(8,128)S(1)} fusion(f32[256,512]{1,0:T(8,128)} %param.4), kind=kOutput, calls=%fused_computation.91 | convolution fusion | flops 805306368 | bytes 1572864 | tf_op jit(solution)/shard_map/dot_general | solution.py:13
  3.0 0.1 all_to_all.16
  3.1 32.7 %all_to_all.24 = f32[64,20,128]{2,1,0:T(8,128)S(1)} all-to-all(f32[64,20,128]{2,1,0:T(8,128)S(1)} %all_to_all.16), channel_id=1, replica_groups=mesh['rows'=64,'chip'=16] {'rows'}, dimensions={0} | all-to-all | bytes 1310720 | tf_op jit(solution)/shard_map/all_to_all | solution.py:26
  35.8 0.1 reduce_sum.18
  35.9 32.3 %all_to_all.25 = f32[16,20,128]{2,1,0:T(8,128)S(1)} all-to-all(f32[16,20,128]{2,1,0:T(8,128)S(1)} %tile.4), channel_id=1, replica_groups=mesh['rows'=64,'chip'=16] {'chip'}, dimensions={0} | all-to-all | bytes 327680 | tf_op jit(solution)/shard_map/all_to_all | solution.py:28
  68.3 0.1 tile.5
  68.3 29.1 %all_to_all.26 = f32[64,20,128]{2,1,0:T(8,128)S(1)} all-to-all(f32[64,20,128]{2,1,0:T(8,128)S(1)} %tile.5), channel_id=1, replica_groups=mesh['rows'=64,'chip'=16] {'rows'}, dimensions={0} | all-to-all | bytes 1310720 | tf_op jit(solution)/shard_map/all_to_all | solution.py:30
  97.5 11.7 %custom-call.12 = f32[128,128]{1,0:T(8,128)S(1)} custom-call(f32[128,128]{1,0:T(8,128)S(1)} %slice.121), custom_call_target="Cholesky" | custom-call | tf_op jit(solution)/shard_map/cholesky/custom-call.1 | solution.py:41
  109.3 0.6 compare_reduce_fusion.3
  109.9 0.7 select_bitcast_fusion.3
  110.6 9.8 %custom-call.13 = f32[1,128,128]{1,2,0:T(8,128)S(1)} custom-call(f32[1,128,128]{2,1,0:T(8,128)S(1)} %get-tuple-element.18), custom_call_target="InvertDiagBlocksLowerTriangular" | custom-call | tf_op jit(solution)/shard_map/triangular_solve/custom-call.0 | solution.py:42
  120.4 0.3 fusion.33
  120.7 0.3 fusion.44
  121.0 0.4 fusion.20
  121.4 0.1 copy.19
  121.5 0.5 convolution_subtract_fusion
  122.0 11.7 %custom-call.14 = f32[128,128]{1,0:T(8,128)S(1)} custom-call(f32[128,128]{1,0:T(8,128)S(1)} %slice.125), custom_call_target="Cholesky" | custom-call | tf_op jit(solution)/shard_map/cholesky/custom-call.1 | solution.py:41
  133.8 0.6 compare_reduce_fusion.2
  134.4 0.7 select_bitcast_fusion.2
  135.1 10.0 %custom-call.15 = f32[1,128,128]{1,2,0:T(8,128)S(1)} custom-call(f32[1,128,128]{2,1,0:T(8,128)S(1)} %get-tuple-element.16), custom_call_target="InvertDiagBlocksLowerTriangular" | custom-call | tf_op jit(solution)/shard_map/triangular_solve/custom-call.0 | solution.py:42
  145.1 0.3 fusion.31
  145.4 0.3 fusion.42
  145.7 0.1 copy.20
  145.8 0.4 convolution_subtract_fusion.4
  146.2 0.3 fusion.61
  146.5 0.6 slice-done.1
  147.1 0.6 convolution_subtract_fusion.2
  147.7 11.7 %custom-call.16 = f32[128,128]{1,0:T(8,128)S(1)} custom-call(f32[128,128]{1,0:T(8,128)S(1)} %slice.128), custom_call_target="Cholesky" | custom-call | tf_op jit(solution)/shard_map/cholesky/custom-call.1 | solution.py:41
  159.4 0.7 compare_reduce_fusion.1
  160.2 0.7 select_bitcast_fusion.1
  160.9 9.8 %custom-call.17 = f32[1,128,128]{1,2,0:T(8,128)S(1)} custom-call(f32[1,128,128]{2,1,0:T(8,128)S(1)} %get-tuple-element.14), custom_call_target="InvertDiagBlocksLowerTriangular" | custom-call | tf_op jit(solution)/shard_map/triangular_solve/custom-call.0 | solution.py:42
  170.7 0.3 fusion.29
  171.0 0.3 fusion.46
  171.3 0.1 copy.21
  171.4 0.7 slice-done
  172.1 0.5 convolution_subtract_fusion.5
  172.6 12.0 %custom-call.18 = f32[128,128]{1,0:T(8,128)S(1)} custom-call(f32[128,128]{1,0:T(8,128)S(1)} %convolution_subtract_fusion.5), custom_call_target="Cholesky" | custom-call | tf_op jit(solution)/shard_map/cholesky/custom-call.1 | solution.py:41
  184.6 0.6 compare_reduce_fusion
  185.3 0.7 select_bitcast_fusion
  185.9 9.8 %custom-call.19 = f32[1,128,128]{1,2,0:T(8,128)S(1)} custom-call(f32[1,128,128]{2,1,0:T(8,128)S(1)} %get-tuple-element.12), custom_call_target="InvertDiagBlocksLowerTriangular" | custom-call | tf_op jit(solution)/shard_map/triangular_solve/custom-call.0 | solution.py:42
  195.7 0.3 fusion.27
  196.1 0.6 convolution_subtract_fusion.3
  196.7 0.3 fusion.62
  197.0 0.8 convolution_subtract_fusion.1
  197.8 0.3 fusion.63
  198.1 1.0 copy.22
  199.1 0.1 fusion.1
  199.2 1.3 copy.23
  (28 shorter events, 0.5 us)
Async XLA Ops:
  97.5 23.2 %copy-start = (f32[256,512]{1,0:T(8,128)S(1)}, f32[256,512]{1,0:T(8,128)}, u32[]{:S(2)}) copy-start(f32[256,512]{1,0:T(8,128)} %param.4) | copy-start | bytes 1572868
  121.4 24.4 %copy-start.1 = (f32[384,128]{0,1:T(8,128)}, f32[384,128]{0,1:T(8,128)S(1)}, u32[]{:S(2)}) copy-start(f32[384,128]{0,1:T(8,128)S(1)} %fusion.20) | copy-start | bytes 589828
  145.7 0.8 copy-start.2
  146.2 0.9 slice-start.1
  171.3 0.8 slice-start
  171.3 0.9 slice-start.2
